TPU v7x, 256 devices: a whole 4x4x8 slice. The times are simulated.
256 devices in a mesh: grp: 32 (over x, z), shard: 8 (over y, core).
Axes of the slice: x: 4, y: 4, z: 8, core: 2. Of those that a mesh axis runs over, the one named last changes fastest.
Arguments:
- layer_inputs: bfloat16 [131072, 1600], P(('grp', 'shard')), may hold values from -6 to 6
- cotangents: bfloat16 [131072, 1600], P(('grp', 'shard')), may hold values from -0.25 to 0.25
- weight: bfloat16 [1600, 1600], P('shard'), may hold values from -0.15625 to 0.15625
- error_state: float32 [32, 1600, 1600], P('grp', 'shard'), may hold values from -6 to 6
- momentum: float32 [1600, 1600], P('shard'), may hold values from -0.75 to 0.75
- bias_momentum: float32 [1600], replicated, may hold values from -6 to 6
- start_basis: float32 [1600, 32], replicated, may hold values from -6 to 6
- next_inputs: bfloat16 [131072, 1600], P(('grp', 'shard')), may hold values from -6 to 6
Outputs:
- next_outputs: bfloat16 [131072, 1600], P(('grp', 'shard'))
- new_error: float32 [32, 1600, 1600], P('grp', 'shard')
- new_momentum: float32 [1600, 1600], P('shard')
- new_bias_momentum: float32 [1600], replicated
All inputs are finite; a program needn't handle non-finite values.
Results may differ from a plain program's by a relative error of at most 0.015.
Values may be sent and summed in bfloat16 or wider, within the bound.
No kernel may reach another device: no remote copies, remote signals or barrier semaphores. Data moves between devices by JAX's collectives and lax.ppermute only.
A program may use at most 128 MiB of HBM per device.

v0:
```python
import jax
import jax.numpy as jnp
from jax import lax
from jax.sharding import PartitionSpec as P

momentum_decay = 0.9
learn_rate = 0.1


def shards(
    layer_inputs, cotangents, weight, error_state, momentum, bias_momentum, start_basis, next_inputs
):
    highest = lax.Precision.HIGHEST
    group_count = lax.axis_size("grp")
    columns = layer_inputs
    gradient = lax.psum_scatter(
        lax.dot_general(
            columns, cotangents, (((0,), (0,)), ((), ())), preferred_element_type=jnp.float32
        ).astype(jnp.bfloat16),
        "shard",
        scatter_dimension=0,
        tiled=True,
    ).astype(jnp.float32)
    column_sums = lax.psum(jnp.sum(cotangents, axis=0, dtype=jnp.float32), ("grp", "shard"))
    corrected = gradient + error_state[0]
    basis = start_basis
    ortho = start_basis
    for round_index in range(2):
        local_factor = jnp.dot(corrected, basis, precision=highest)
        own_rows = lax.psum(local_factor, "grp")
        gram = lax.psum(jnp.dot(own_rows.T, own_rows, precision=highest), "shard")
        lower_factor = jnp.linalg.cholesky(gram)
        ortho = jax.scipy.linalg.solve_triangular(lower_factor, own_rows.T, lower=True).T
        partial_basis = lax.dot_general(
            corrected, ortho, (((0,), (0,)), ((), ())), precision=highest
        )
        summed = lax.psum(partial_basis, ("grp", "shard"))
        basis = summed / group_count
    approx = jnp.dot(ortho, basis.T, precision=highest)
    new_error = (corrected - approx)[None, :, :]
    new_momentum = momentum_decay * momentum + approx
    new_bias_momentum = momentum_decay * bias_momentum + column_sums / group_count
    new_weight = (weight.astype(jnp.float32) - learn_rate * new_momentum).astype(jnp.bfloat16)
    columns = next_inputs
    projected = jnp.dot(
        columns,
        lax.all_gather(new_weight, "shard", axis=0, tiled=True),
        preferred_element_type=jnp.float32,
    )
    return (projected.astype(jnp.bfloat16), new_error, new_momentum, new_bias_momentum)


def solution(mesh):
    placed = (
        P(("grp", "shard"), None),
        P(("grp", "shard"), None),
        P("shard", None),
        P("grp", "shard", None),
        P("shard", None),
        P(),
        P(),
        P(("grp", "shard"), None),
    )
    return jax.shard_map(
        shards,
        mesh=mesh,
        in_specs=placed,
        out_specs=(P(("grp", "shard"), None), P("grp", "shard", None), P("shard", None), P()),
        check_vma=False,
    )
```

profile of v0, /device:TPU:1, one launch (start us, length us, event | category | flops | bytes accessed | tf_op | source)
XLA Modules:
  0.0 1017.4 jit_solution(5363052511592432300)
XLA Ops:
  7.2 0.0 copy-start
  7.2 0.0 reduce-scatter.4.cloned.1.call-start
  7.2 1.4 copy-done
  8.6 6.3 convolution_convert_fusion
  14.9 0.0 copy-start.1
  14.9 0.0 copy-start.2
  14.9 0.0 reduce-scatter.4.cloned.1.call-update
  15.0 0.0 all-reduce.4.cloned.1.call-start
  15.0 50.3 %reduce-scatter.4.cloned.1.call-done = bf16[200,1600]{1,0:T(8,128)(2,1)} async-done(((bf16[1600,1600]{1,0:T(8,128)(2,1)}), bf16[200,1600]{1,0:T(8,128)(2,1)}) %reduce-scatter.4.cloned.1.call-update) | async-done | bytes 640016
  65.3 0.0 copy-done.1
  65.3 0.0 copy-done.2
  65.3 2.4 fusion.23
  67.8 115.4 %psum.49 = f32[200,32]{0,1:T(8,128)S(1)} all-reduce(f32[200,32]{0,1:T(8,128)S(1)} %fusion.23), channel_id=1, replica_groups=mesh['grp'=32,'shard'=8] {'grp'}, use_global_device_ids=true, to_apply=%region_1.0 | all-reduce | flops 6400 | bytes 51200 | tf_op jit(solution)/shard_map/psum | solution.py:30
  183.2 0.2 fusion.26
  183.4 51.6 %psum.50 = f32[32,32]{0,1:T(8,128)S(1)} all-reduce(f32[32,32]{0,1:T(8,128)S(1)} %fusion.26), channel_id=1, replica_groups=mesh['grp'=32,'shard'=8] {'shard'}, use_global_device_ids=true, to_apply=%region_2.0 | all-reduce | flops 1024 | bytes 8192 | tf_op jit(solution)/shard_map/psum | solution.py:31
  234.9 0.1 copy.17
  235.0 2.9 cholesky.44
  238.0 0.6 compare_reduce_fusion.1
  238.6 0.7 fusion.11
  239.3 2.4 custom-call.6
  241.7 0.2 fusion.9
  242.0 4.8 fusion.22
  246.7 0.0 all-reduce.4.cloned.1.call-update
  246.8 0.0 all-reduce.6.cloned.1.call-start
  246.8 248.4 %all-reduce.4.cloned.1.call-done = f32[1600,32]{1,0:T(8,128)} async-done(((f32[1600,32]{1,0:T(8,128)}), f32[1600,32]{1,0:T(8,128)}) %all-reduce.4.cloned.1.call-update) | async-done | bytes 204816 | tf_op jit(solution)/shard_map/psum | solution.py:37
  495.2 2.9 fusion.3
  498.1 114.1 %psum.52 = f32[200,32]{0,1:T(8,128)S(1)} all-reduce(f32[200,32]{0,1:T(8,128)S(1)} %fusion.3), channel_id=1, replica_groups=mesh['grp'=32,'shard'=8] {'grp'}, use_global_device_ids=true, to_apply=%region_6.0 | all-reduce | flops 6400 | bytes 51200 | tf_op jit(solution)/shard_map/psum | solution.py:30
  612.2 0.2 fusion.27
  612.4 46.1 %psum.53 = f32[32,32]{0,1:T(8,128)S(1)} all-reduce(f32[32,32]{0,1:T(8,128)S(1)} %fusion.27), channel_id=1, replica_groups=mesh['grp'=32,'shard'=8] {'shard'}, use_global_device_ids=true, to_apply=%region_7.0 | all-reduce | flops 1024 | bytes 8192 | tf_op jit(solution)/shard_map/psum | solution.py:31
  658.5 0.1 copy.19
  658.6 2.9 cholesky.55
  661.6 0.6 compare_reduce_fusion
  662.2 0.7 fusion.12
  662.9 2.4 custom-call.7
  665.3 0.2 fusion.7
  665.5 4.8 fusion.21
  670.3 0.0 all-reduce.6.cloned.1.call-update
  670.4 0.0 all-gather.2.cloned.1.call-start
  670.4 248.4 %all-reduce.6.cloned.1.call-done = f32[1600,32]{1,0:T(8,128)} async-done(((f32[1600,32]{1,0:T(8,128)}), f32[1600,32]{1,0:T(8,128)}) %all-reduce.6.cloned.1.call-update) | async-done | bytes 204816 | tf_op jit(solution)/shard_map/psum | solution.py:37
  918.8 5.3 subtract_convert_fusion
  924.0 0.0 copy-start.3
  924.1 0.0 all-gather.2.cloned.1.call-update
  924.1 1.7 convert_reduce_fusion
  925.8 77.1 %psum.55 = f32[1600]{0:T(1024)S(1)} all-reduce(f32[1600]{0:T(1024)S(1)} %convert_reduce_fusion), channel_id=1, replica_groups=mesh['grp'=32,'shard'=8] {'grp','shard'}, use_global_device_ids=true, to_apply=%region_10.13 | all-reduce | flops 1600 | bytes 12800 | tf_op jit(solution)/shard_map/psum | solution.py:24
  1002.9 0.0 copy-done.3
  1002.9 0.6 multiply_add_fusion.1
  1003.5 0.0 all-gather.2.cloned.1.call-done
  1003.5 7.4 fusion
  (4 shorter events, 0.1 us)
Async XLA Ops:
  7.2 1.4 copy-start
  7.2 58.1 %reduce-scatter.4.cloned.1.call-start = ((), (), s32[]{:S(2)}) async-start(), calls=%async_computation.4 | async-start | bytes 5990400
  14.9 50.4 %copy-start.1 = (f32[1,200,1600]{2,1,0:T(8,128)S(1)}, f32[1,200,1600]{2,1,0:T(8,128)}, u32[]{:S(2)}) copy-start(f32[1,200,1600]{2,1,0:T(8,128)} %param.14) | copy-start | bytes 3840004
  14.9 50.4 %copy-start.2 = (f32[1600,32]{0,1:T(8,128)S(1)}, f32[1600,32]{0,1:T(8,128)}, u32[]{:S(2)}) copy-start(f32[1600,32]{0,1:T(8,128)} %param.17) | copy-start | bytes 614404
  15.0 480.3 %all-reduce.4.cloned.1.call-start = ((), (), s32[]{:S(2)}) async-start(), calls=%async_computation.1 | async-start | bytes 1638400 | tf_op jit(solution)/shard_map/psum | solution.py:37
  246.8 672.0 %all-reduce.6.cloned.1.call-start = ((), (), s32[]{:S(2)}) async-start(), calls=%async_computation.2 | async-start | bytes 1638400 | tf_op jit(solution)/shard_map/psum | solution.py:37
  670.4 333.1 %all-gather.2.cloned.1.call-start = ((), (), s32[]{:S(2)}) async-start(), calls=%async_computation.3 | async-start | bytes 5990400 | tf_op jit(solution)/shard_map/all_gather | solution.py:47
  924.0 78.8 %copy-start.3 = (f32[1600]{0:T(1024)S(1)}, f32[1600]{0:T(1024)}, u32[]{:S(2)}) copy-start(f32[1600]{0:T(1024)} %param.16) | copy-start | bytes 19204
Sparse Core Ops, SparseCore 0:
  15.1 50.1 reduce-scatter.3
  246.9 248.2 all-reduce.3
  670.5 248.2 all-reduce.5
  924.2 38.9 all-gather.1
where the time goes:
time: 1020 us
  waiting for transfers between devices  547 us (54%)
  blocking collectives  404 us (40%)
  matrix products  34.6 us (3%)
  other arithmetic  15.7 us (2%)
  between operations  13.8 us (1%)
    psum x2, waiting for transfers between devices, shards(): summed = lax.psum(partial_basis, ('grp', 'shard'))  497 us
    psum x2, blocking collectives, shards(): own_rows = lax.psum(local_factor, 'grp')  230 us
    psum x2, blocking collectives, shards(): gram = lax.psum(jnp.dot(own_rows.T, own_rows, precision=highest), 'shard')  97.7 us
    psum x1, blocking collectives, shards(): lax.psum(jnp.sum(cotangents, axis=0, dtype=jnp.float32), ('grp', 'shard'))  77.1 us
    unnamed x5, waiting for transfers between devices  50.4 us
  transfers between devices with their start and end apart: 4, of which 3 were waited for; matrix products, arithmetic and copies ran while one was open for 0% of the time, Pallas kernels for 0%

commit v1 on v0

v1 whole, which is shorter than its diff:
```python
import jax
import jax.numpy as jnp
from jax import lax
from jax.sharding import PartitionSpec as P

momentum_decay = 0.9
learn_rate = 0.1


def shards(
    layer_inputs, cotangents, weight, error_state, momentum, bias_momentum, start_basis, next_inputs
):
    highest = lax.Precision.HIGHEST
    group_count = lax.axis_size("grp")
    rank = start_basis.shape[1]
    gradient = lax.psum_scatter(
        lax.dot_general(
            layer_inputs, cotangents, (((0,), (0,)), ((), ())), preferred_element_type=jnp.float32
        ).astype(jnp.bfloat16),
        "shard",
        scatter_dimension=0,
        tiled=True,
    ).astype(jnp.float32)
    column_sums = jnp.sum(cotangents, axis=0, dtype=jnp.float32)
    corrected = gradient + error_state[0]
    summed = lax.psum(jnp.concatenate([corrected, column_sums[None, :]], axis=0), "grp")
    total = summed[:-1]
    grp_sums = summed[-1]
    basis = start_basis
    ortho = start_basis
    for round_index in range(2):
        factor = jnp.dot(total, basis, precision=highest)
        gram_part = jnp.dot(factor.T, factor, precision=highest)
        if round_index == 0:
            packed = lax.psum(jnp.concatenate([gram_part.reshape(-1), grp_sums]), "shard")
            gram = packed[: rank * rank].reshape(rank, rank)
            all_sums = packed[rank * rank :]
        else:
            gram = lax.psum(gram_part, "shard")
        lower_factor = jnp.linalg.cholesky(gram)
        ortho = jax.scipy.linalg.solve_triangular(lower_factor, factor.T, lower=True).T
        partial_basis = lax.dot_general(
            total, ortho, (((0,), (0,)), ((), ())), precision=highest
        )
        basis = lax.psum(partial_basis, "shard") / group_count
    approx = jnp.dot(ortho, basis.T, precision=highest)
    new_error = (corrected - approx)[None, :, :]
    new_momentum = momentum_decay * momentum + approx
    new_bias_momentum = momentum_decay * bias_momentum + all_sums / group_count
    new_weight = (weight.astype(jnp.float32) - learn_rate * new_momentum).astype(jnp.bfloat16)
    projected = jnp.dot(
        next_inputs,
        lax.all_gather(new_weight, "shard", axis=0, tiled=True),
        preferred_element_type=jnp.float32,
    )
    return (projected.astype(jnp.bfloat16), new_error, new_momentum, new_bias_momentum)


def solution(mesh):
    placed = (
        P(("grp", "shard"), None),
        P(("grp", "shard"), None),
        P("shard", None),
        P("grp", "shard", None),
        P("shard", None),
        P(),
        P(),
        P(("grp", "shard"), None),
    )
    return jax.shard_map(
        shards,
        mesh=mesh,
        in_specs=placed,
        out_specs=(P(("grp", "shard"), None), P("grp", "shard", None), P("shard", None), P()),
        check_vma=False,
    )
```

time: 1020 us -> 474 us (0.46)
  blocking collectives: 404 us -> 47.7 us
  waiting for transfers between devices: 547 us -> 362 us
    psum x5 -> x2, blocking collectives: 404 us -> 47.7 us  [the longest x1 25.7 us: shards(): lax.psum(jnp.concatenate([gram_part.reshape(-1), grp_sums]), 'shard')]
    psum x2 -> x3, waiting for transfers between devices: 497 us -> 275 us  [the longest x1 149 us: shards(): lax.psum(jnp.concatenate([corrected, column_sums[None, :]], axis=0), 'grp')]
    all_gather x1, waiting for transfers between devices: 0.01 us -> 38.7 us  [shards(): lax.all_gather(new_weight, 'shard', axis=0, tiled=True)]
    unnamed x5 -> x6, waiting for transfers between devices: 50.4 us -> 48.8 us
  transfers between devices with their start and end apart: 4 -> 5, of which waited for: 3 -> 5; matrix products, arithmetic and copies ran while one was open for 0% -> 0% of each run, Pallas kernels for 0% -> 0%
where the time goes in v1:
time: 474 us; the launch traced here: 473 us
  waiting for transfers between devices  362 us (76%)
  blocking collectives  47.7 us (10%)
  matrix products  28.1 us (6%)
  other arithmetic  17.1 us (4%)
  between operations  13.9 us (3%)
    psum x1, waiting for transfers between devices, shards(): lax.psum(jnp.concatenate([corrected, column_sums[None, :]], axis=0), 'grp')  149 us
    psum x2, waiting for transfers between devices, shards(): basis = lax.psum(partial_basis, 'shard') / group_count  125 us
    unnamed x6, waiting for transfers between devices  48.8 us
    all_gather x1, waiting for transfers between devices, shards(): lax.all_gather(new_weight, 'shard', axis=0, tiled=True)  38.7 us
    psum x1, blocking collectives, shards(): lax.psum(jnp.concatenate([gram_part.reshape(-1), grp_sums]), 'shard')  25.7 us
    psum x1, blocking collectives, shards(): gram = lax.psum(gram_part, 'shard')  21.9 us
  transfers between devices with their start and end apart: 5, of which 5 were waited for; matrix products, arithmetic and copies ran while one was open for 0% of the time, Pallas kernels for 0%

profile of v1, /device:TPU:1, one launch (start us, length us, event | category | flops | bytes accessed | tf_op | source)
XLA Modules:
  0.0 473.4 jit_solution(3598170805652788617)
XLA Ops:
  7.2 0.0 copy-start
  7.2 0.0 reduce-scatter.4.cloned.1.call-start
  7.2 1.4 copy-done
  8.6 6.3 %convolution_convert_fusion = bf16[1600,1600]{1,0:T(8,128)(2,1)} fusion(bf16[512,1600]{0,1:T(8,128)(2,1)S(1)} %copy-done, bf16[512,1600]{0,1:T(8,128)(2,1)} %param.12), kind=kOutput, calls=%fused_computation | convolution fusion | flops 2624000000 | bytes 8396800 | tf_op jit(solution)/shard_map/dot_general | solution.py:17
  14.9 0.0 reduce-scatter.4.cloned.1.call-update
  14.9 0.0 all-reduce.5.cloned.1.call-start
  15.0 1.4 copy-done.3
  16.4 0.3 convert_reduce_fusion
  16.7 48.7 %reduce-scatter.4.cloned.1.call-done = bf16[200,1600]{1,0:T(8,128)(2,1)} async-done(((bf16[1600,1600]{1,0:T(8,128)(2,1)}), bf16[200,1600]{1,0:T(8,128)(2,1)}) %reduce-scatter.4.cloned.1.call-update) | async-done | bytes 640016
  65.4 1.6 bitcast_add_fusion
  67.0 1.1 copy-done.2
  68.1 1.2 pad_maximum_fusion
  69.3 0.0 all-reduce.5.cloned.1.call-update
  69.3 0.0 all-reduce.7.cloned.1.call-start
  69.3 149.4 %all-reduce.5.cloned.1.call-done = f32[201,1600]{1,0:T(8,128)} async-done(((f32[201,1600]{1,0:T(8,128)}), f32[201,1600]{1,0:T(8,128)}) %all-reduce.5.cloned.1.call-update) | async-done | bytes 1286416 | tf_op jit(solution)/shard_map/psum | solution.py:26
  218.7 2.8 fusion.7
  221.5 0.2 fusion.31
  221.7 0.1 reshape.30
  221.8 25.7 %psum.36 = f32[2624]{0:T(1024)S(1)} all-reduce(f32[2624]{0:T(1024)S(1)} %pad_maximum_fusion.1), channel_id=1, replica_groups=mesh['grp'=32,'shard'=8] {'shard'}, use_global_device_ids=true, to_apply=%region_3.0 | all-reduce | flops 2624 | bytes 20992 | tf_op jit(solution)/shard_map/psum | solution.py:35
  247.5 0.1 reshape.31
  247.6 0.1 copy.18
  247.7 2.9 cholesky.44
  250.6 0.6 compare_reduce_fusion.1
  251.3 0.7 fusion.18
  251.9 2.4 custom-call.6
  254.4 0.2 fusion.16
  254.6 1.7 fusion.5
  256.3 0.0 all-reduce.7.cloned.1.call-update
  256.3 0.0 all-reduce.9.cloned.1.call-start
  256.4 60.6 %all-reduce.7.cloned.1.call-done = f32[1600,32]{0,1:T(8,128)} async-done(((f32[1600,32]{0,1:T(8,128)}), f32[1600,32]{0,1:T(8,128)}) %all-reduce.7.cloned.1.call-update) | async-done | bytes 204816 | tf_op jit(solution)/shard_map/psum | solution.py:45
  317.0 2.3 fusion.3
  319.2 0.2 fusion.32
  319.4 21.9 %psum.38 = f32[32,32]{0,1:T(8,128)S(1)} all-reduce(f32[32,32]{0,1:T(8,128)S(1)} %fusion.32), channel_id=1, replica_groups=mesh['grp'=32,'shard'=8] {'shard'}, use_global_device_ids=true, to_apply=%region_7.10 | all-reduce | flops 1024 | bytes 8192 | tf_op jit(solution)/shard_map/psum | solution.py:39
  341.3 0.1 copy.20
  341.4 2.9 cholesky.55
  344.4 0.6 compare_reduce_fusion
  345.0 0.7 fusion.19
  345.7 2.4 custom-call.7
  348.1 0.2 fusion.14
  348.3 1.7 fusion.1
  350.0 0.0 all-reduce.9.cloned.1.call-update
  350.0 0.0 all-gather.2.cloned.1.call-start
  350.1 64.9 %all-reduce.9.cloned.1.call-done = f32[1600,32]{0,1:T(8,128)} async-done(((f32[1600,32]{0,1:T(8,128)}), f32[1600,32]{0,1:T(8,128)}) %all-reduce.9.cloned.1.call-update) | async-done | bytes 204816 | tf_op jit(solution)/shard_map/psum | solution.py:45
  415.0 5.2 %subtract_convert_fusion = (bf16[200,1600]{1,0:T(8,128)(2,1)}, f32[200,1600]{1,0:T(8,128)}, f32[1,200,1600]{2,1,0:T(8,128)}) fusion(bf16[200,1600]{1,0:T(8,128)(2,1)} %param.13, f32[200,1600]{1,0:T(8,128)} %param.15, f32[200,1600]{1,0:T(8,128)} %copy-done.2, f32[32,200]{1,0:T(8,128)S(1)} %fusion.14, f32[1600,32]{0,1:T(8,128)} %all-reduce.9.cloned.1.call-done), kind=kOutput, calls=%fused_computation.7 | convolution fusion | flops 125171200 | bytes 6630400 | tf_op jit(solution)/shard_map/dot_general | solution.py:46
  420.2 0.0 all-gather.2.cloned.1.call-update
  420.2 0.6 fusion.26
  420.8 38.7 %all-gather.2.cloned.1.call-done = bf16[1600,1600]{1,0:T(8,128)(2,1)} async-done(((bf16[200,1600]{1,0:T(8,128)(2,1)}), bf16[1600,1600]{1,0:T(8,128)(2,1)}) %all-gather.2.cloned.1.call-update) | async-done | bytes 5120016 | tf_op jit(solution)/shard_map/all_gather | solution.py:53
  459.5 7.4 %fusion = bf16[512,1600]{0,1:T(8,128)(2,1)} fusion(bf16[1600,1600]{1,0:T(8,128)(2,1)} %all-gather.2.cloned.1.call-done, bf16[512,1600]{0,1:T(8,128)(2,1)} %param.18), kind=kOutput, calls=%fused_computation.3 | convolution fusion | flops 2622259200 | bytes 8396800 | tf_op jit(solution)/shard_map/dot_general | solution.py:51
  (16 shorter events, 0.1 us)
Async XLA Ops:
  7.2 1.4 copy-start
  7.2 58.2 %reduce-scatter.4.cloned.1.call-start = ((), (), s32[]{:S(2)}) async-start(), calls=%async_computation.5 | async-start | bytes 5990400
  14.9 1.4 copy-start.3
  14.9 203.7 %all-reduce.5.cloned.1.call-start = ((), (), s32[]{:S(2)}) async-start(), calls=%async_computation.1 | async-start | bytes 2768896 | tf_op jit(solution)/shard_map/psum | solution.py:26
  67.0 1.1 copy-start.2
  68.1 150.6 %copy-start.4 = (f32[1600,32]{0,1:T(8,128)S(1)}, f32[1600,32]{0,1:T(8,128)}, u32[]{:S(2)}) copy-start(f32[1600,32]{0,1:T(8,128)} %param.17) | copy-start | bytes 614404
  69.3 247.7 %all-reduce.7.cloned.1.call-start = ((), (), s32[]{:S(2)}) async-start(), calls=%async_computation.2 | async-start | bytes 425984 | tf_op jit(solution)/shard_map/psum | solution.py:45
  218.7 3.0 copy-start.1
  256.3 158.7 %all-reduce.9.cloned.1.call-start = ((), (), s32[]{:S(2)}) async-start(), calls=%async_computation.3 | async-start | bytes 425984 | tf_op jit(solution)/shard_map/psum | solution.py:45
  350.0 70.2 %copy-start.5 = (f32[1600]{0:T(1024)S(1)}, f32[1600]{0:T(1024)}, u32[]{:S(2)}) copy-start(f32[1600]{0:T(1024)} %param.16) | copy-start | bytes 19204
  350.0 109.5 %all-gather.2.cloned.1.call-start = ((), (), s32[]{:S(2)}) async-start(), calls=%async_computation.4 | async-start | bytes 5990400 | tf_op jit(solution)/shard_map/all_gather | solution.py:53
Sparse Core Ops, SparseCore 0:
  15.1 50.2 reduce-scatter.3
  69.4 149.1 all-reduce.4
  256.4 60.4 all-reduce.6
  350.1 64.7 all-reduce.8
  420.3 39.1 all-gather.1

commit v2 on v1

--- a/solution.py
+++ b/solution.py
@@ -12,7 +12,7 @@
 ):
     highest = lax.Precision.HIGHEST
     group_count = lax.axis_size("grp")
-    rank = start_basis.shape[1]
+    shard_count = lax.axis_size("shard")
     gradient = lax.psum_scatter(
         lax.dot_general(
             layer_inputs, cotangents, (((0,), (0,)), ((), ())), preferred_element_type=jnp.float32
@@ -23,27 +23,25 @@
     ).astype(jnp.float32)
     column_sums = jnp.sum(cotangents, axis=0, dtype=jnp.float32)
     corrected = gradient + error_state[0]
+    own_rows = corrected.shape[0]
+    block = own_rows + 1
     summed = lax.psum(jnp.concatenate([corrected, column_sums[None, :]], axis=0), "grp")
-    total = summed[:-1]
-    grp_sums = summed[-1]
+    extended = lax.all_gather(summed, "shard", axis=0, tiled=True)
+    all_sums = jnp.sum(extended.reshape(shard_count, block, -1)[:, own_rows], axis=0)
+    is_total_row = (jnp.arange(shard_count * block) % block < own_rows)[:, None]
     basis = start_basis
     ortho = start_basis
     for round_index in range(2):
-        factor = jnp.dot(total, basis, precision=highest)
-        gram_part = jnp.dot(factor.T, factor, precision=highest)
-        if round_index == 0:
-            packed = lax.psum(jnp.concatenate([gram_part.reshape(-1), grp_sums]), "shard")
-            gram = packed[: rank * rank].reshape(rank, rank)
-            all_sums = packed[rank * rank :]
-        else:
-            gram = lax.psum(gram_part, "shard")
+        factor = jnp.where(is_total_row, jnp.dot(extended, basis, precision=highest), 0.0)
+        gram = jnp.dot(factor.T, factor, precision=highest)
         lower_factor = jnp.linalg.cholesky(gram)
         ortho = jax.scipy.linalg.solve_triangular(lower_factor, factor.T, lower=True).T
-        partial_basis = lax.dot_general(
-            total, ortho, (((0,), (0,)), ((), ())), precision=highest
+        basis = (
+            lax.dot_general(extended, ortho, (((0,), (0,)), ((), ())), precision=highest)
+            / group_count
         )
-        basis = lax.psum(partial_basis, "shard") / group_count
-    approx = jnp.dot(ortho, basis.T, precision=highest)
+    own_ortho = lax.dynamic_slice_in_dim(ortho, lax.axis_index("shard") * block, own_rows, axis=0)
+    approx = jnp.dot(own_ortho, basis.T, precision=highest)
     new_error = (corrected - approx)[None, :, :]
     new_momentum = momentum_decay * momentum + approx
     new_bias_momentum = momentum_decay * bias_momentum + all_sums / group_count

time: 474 us -> 410 us (0.86)
  waiting for transfers between devices: 362 us -> 305 us
  blocking collectives: 47.7 us -> 0 us
  matrix products: 28.1 us -> 60.4 us
  local copies, waits for them, and re-layouts: 4.13 us -> 10.9 us
    psum x2 -> x0, waiting for transfers between devices: 125 us -> none  [shards(): basis = lax.psum(partial_basis, 'shard') / group_count]
    all_gather x0 -> x1, waiting for transfers between devices: none -> 67.5 us  [shards(): extended = lax.all_gather(summed, 'shard', axis=0, tiled=True)]
    psum x2 -> x0, blocking collectives: 47.7 us -> none  [the longest x1 25.7 us: shards(): lax.psum(jnp.concatenate([gram_part.reshape(-1), grp_sums]), 'shard')]
    dot_general x7, matrix products: 13.9 us -> 45.9 us  [the longest x2 22.8 us: shards(): jnp.dot(extended, basis, precision=highest)]
    unnamed x12 -> x13, local copies, waits for them, and re-layouts: 3.81 us -> 10.8 us
    unnamed x6 -> x5, waiting for transfers between devices: 48.8 us -> 48.6 us
  transfers between devices with their start and end apart: 5 -> 4, of which waited for: 5 -> 4; matrix products, arithmetic and copies ran while one was open for 0% -> 1% of each run, Pallas kernels for 0% -> 0%
where the time goes in v2:
time: 410 us
  waiting for transfers between devices  305 us (74%)
  matrix products  60.4 us (15%)
  other arithmetic  19.6 us (5%)
  between operations  13.9 us (3%)
  local copies, waits for them, and re-layouts  10.9 us (3%)
    psum x1, waiting for transfers between devices, shards(): lax.psum(jnp.concatenate([corrected, column_sums[None, :]], axis=0), 'grp')  150 us
    all_gather x1, waiting for transfers between devices, shards(): extended = lax.all_gather(summed, 'shard', axis=0, tiled=True)  67.5 us
    unnamed x5, waiting for transfers between devices  48.6 us
    all_gather x1, waiting for transfers between devices, shards(): lax.all_gather(new_weight, 'shard', axis=0, tiled=True)  38.2 us
    dot_general x2, matrix products, shards(): jnp.dot(extended, basis, precision=highest)  22.8 us
    dot_general x2, matrix products, shards(): lax.dot_general(extended, ortho, (((0,), (0,)), ((), ())), precision=high...  19.1 us
    unnamed x13, local copies, waits for them, and re-layouts  10.8 us
  transfers between devices with their start and end apart: 4, of which 4 were waited for; matrix products, arithmetic and copies ran while one was open for 1% of the time, Pallas kernels for 0%

profile of v2, /device:TPU:1, one launch (start us, length us, event | category | flops | bytes accessed | tf_op | source)
XLA Modules:
  0.0 409.5 jit_solution(4869989096290573396)
XLA Ops:
  7.2 0.0 copy-start
  7.2 0.0 reduce-scatter.4.cloned.1.call-start
  7.2 1.4 copy-done
  8.6 6.3 %convolution_convert_fusion = bf16[1600,1600]{1,0:T(8,128)(2,1)} fusion(bf16[512,1600]{0,1:T(8,128)(2,1)S(1)} %copy-done, bf16[512,1600]{0,1:T(8,128)(2,1)} %param.12), kind=kOutput, calls=%fused_computation | convolution fusion | flops 2624000000 | bytes 8396800 | tf_op jit(solution)/shard_map/dot_general | solution.py:17
  14.9 0.0 reduce-scatter.4.cloned.1.call-update
  14.9 0.0 all-reduce.3.cloned.1.call-start
  15.0 1.7 convert_reduce_fusion
  16.8 48.5 %reduce-scatter.4.cloned.1.call-done = bf16[200,1600]{1,0:T(8,128)(2,1)} async-done(((bf16[1600,1600]{1,0:T(8,128)(2,1)}), bf16[200,1600]{1,0:T(8,128)(2,1)}) %reduce-scatter.4.cloned.1.call-update) | async-done | bytes 640016
  65.3 1.6 bitcast_add_fusion
  66.9 1.2 pad_maximum_fusion
  68.1 0.0 all-reduce.3.cloned.1.call-update
  68.1 0.0 all-gather.6.cloned.1.call-start
  68.2 150.3 %all-reduce.3.cloned.1.call-done = f32[201,1600]{1,0:T(8,128)} async-done(((f32[201,1600]{1,0:T(8,128)}), f32[201,1600]{1,0:T(8,128)}) %all-reduce.3.cloned.1.call-update) | async-done | bytes 1286416 | tf_op jit(solution)/shard_map/psum | solution.py:28
  218.5 0.0 all-gather.6.cloned.1.call-update
  218.5 0.0 all-gather.4.cloned.1.call-start
  218.6 0.0 copy-start.4
  218.6 67.5 %all-gather.6.cloned.1.call-done = f32[8,201,1600]{2,1,0:T(8,128)} async-done(((f32[1,201,1600]{2,1,0:T(8,128)}), f32[8,201,1600]{2,1,0:T(8,128)}) %all-gather.6.cloned.1.call-update) | async-done | bytes 10291216 | tf_op jit(solution)/shard_map/all_gather | solution.py:29
  286.1 9.4 %reshape.31 = f32[1608,1600]{1,0:T(8,128)} reshape(f32[8,201,1600]{2,1,0:T(8,128)} %all-gather.6.cloned.1.call-done) | data formatting | bytes 20582400
  295.4 0.0 copy-done.4
  295.4 13.2 %convolution_select_fusion.1 = f32[1608,32]{0,1:T(8,128)S(1)} fusion(f32[1608,1600]{1,0:T(8,128)} %reshape.31, f32[1600,32]{0,1:T(8,128)S(1)} %copy-done.4, pred[1608]{0:T(1024)(128)(4,1)S(1)} %fusion.15), kind=kOutput, calls=%fused_computation.5 | convolution fusion | flops 988006656 | bytes 10703432 | tf_op jit(solution)/shard_map/dot_general | solution.py:35
  308.6 0.3 fusion.22
  309.0 0.1 copy.16
  309.0 2.9 cholesky.44
  312.0 0.6 compare_reduce_fusion.1
  312.6 0.7 fusion.7
  313.3 2.4 custom-call.6
  315.7 0.4 fusion.3
  316.2 0.0 copy-start.1
  316.2 9.6 %convolution_multiply_fusion.1 = f32[1600,32]{0,1:T(8,128)S(1)} fusion(f32[1608,1600]{1,0:T(8,128)} %reshape.31, f32[32,1608]{1,0:T(8,128)S(1)} %fusion.3), kind=kOutput, calls=%fused_computation.7 | convolution fusion | flops 988006400 | bytes 10701824 | tf_op jit(solution)/shard_map/dot_general | solution.py:40
  325.7 0.0 copy-done.1
  325.7 9.6 %convolution_select_fusion = f32[1608,32]{0,1:T(8,128)S(1)} fusion(f32[1608,1600]{1,0:T(8,128)S(1)} %copy-done.1, f32[1600,32]{0,1:T(8,128)S(1)} %convolution_multiply_fusion.1, pred[1608]{0:T(1024)(128)(4,1)S(1)} %fusion.15), kind=kOutput, calls=%fused_computation.4 | convolution fusion | flops 988006656 | bytes 10703432 | tf_op jit(solution)/shard_map/dot_general | solution.py:35
  335.3 0.3 fusion.23
  335.6 0.1 copy.17
  335.7 2.9 cholesky.55
  338.7 0.6 compare_reduce_fusion
  339.3 0.7 fusion.8
  340.0 2.4 custom-call.7
  342.4 0.4 fusion.1
  342.8 0.0 copy-start.2
  342.8 0.0 copy-start.3
  342.9 9.6 %convolution_multiply_fusion = f32[1600,32]{0,1:T(8,128)S(1)} fusion(f32[1608,1600]{1,0:T(8,128)} %reshape.31, f32[32,1608]{1,0:T(8,128)S(1)} %fusion.1), kind=kOutput, calls=%fused_computation.6 | convolution fusion | flops 988006400 | bytes 10701824 | tf_op jit(solution)/shard_map/dot_general | solution.py:40
  352.5 0.0 copy-start.5
  352.5 3.3 subtract_convert_fusion
  355.8 0.0 all-gather.4.cloned.1.call-update
  355.8 1.0 slice_reduce_fusion
  356.9 0.6 multiply_add_fusion.1
  357.5 38.2 %all-gather.4.cloned.1.call-done = bf16[1600,1600]{1,0:T(8,128)(2,1)} async-done(((bf16[200,1600]{1,0:T(8,128)(2,1)}), bf16[1600,1600]{1,0:T(8,128)(2,1)}) %all-gather.4.cloned.1.call-update) | async-done | bytes 5120016 | tf_op jit(solution)/shard_map/all_gather | solution.py:51
  395.7 7.4 %fusion = bf16[512,1600]{0,1:T(8,128)(2,1)} fusion(bf16[1600,1600]{1,0:T(8,128)(2,1)} %all-gather.4.cloned.1.call-done, bf16[512,1600]{0,1:T(8,128)(2,1)} %param.18), kind=kOutput, calls=%fused_computation.3 | convolution fusion | flops 2622259200 | bytes 8396800 | tf_op jit(solution)/shard_map/dot_general | solution.py:49
  (9 shorter events, 0.1 us)
Async XLA Ops:
  7.2 1.4 copy-start
  7.2 58.1 %reduce-scatter.4.cloned.1.call-start = ((), (), s32[]{:S(2)}) async-start(), calls=%async_computation.4 | async-start | bytes 5990400
  14.9 203.6 %all-reduce.3.cloned.1.call-start = ((), (), s32[]{:S(2)}) async-start(), calls=%async_computation.1 | async-start | bytes 2768896 | tf_op jit(solution)/shard_map/psum | solution.py:28
  68.1 218.0 %all-gather.6.cloned.1.call-start = ((), (), s32[]{:S(2)}) async-start(), calls=%async_computation.3 | async-start | bytes 12460032 | tf_op jit(solution)/shard_map/all_gather | solution.py:29
  218.5 177.1 %all-gather.4.cloned.1.call-start = ((), (), s32[]{:S(2)}) async-start(), calls=%async_computation.2 | async-start | bytes 5990400 | tf_op jit(solution)/shard_map/all_gather | solution.py:51
  218.6 76.8 %copy-start.4 = (f32[1600,32]{0,1:T(8,128)S(1)}, f32[1600,32]{0,1:T(8,128)}, u32[]{:S(2)}) copy-start(f32[1600,32]{0,1:T(8,128)} %param.17) | copy-start | bytes 614404
  316.2 9.6 %copy-start.1 = (f32[1608,1600]{1,0:T(8,128)S(1)}, f32[1608,1600]{1,0:T(8,128)}, u32[]{:S(2)}) copy-start(f32[1608,1600]{1,0:T(8,128)} %reshape.31) | copy-start | bytes 30873604
  342.8 9.6 %copy-start.2 = (f32[200,1600]{1,0:T(8,128)S(1)}, f32[200,1600]{1,0:T(8,128)}, u32[]{:S(2)}) copy-start(f32[200,1600]{1,0:T(8,128)} %param.15) | copy-start | bytes 3840004
  342.8 9.6 %copy-start.3 = (bf16[200,1600]{1,0:T(8,128)(2,1)S(1)}, bf16[200,1600]{1,0:T(8,128)(2,1)}, u32[]{:S(2)}) copy-start(bf16[200,1600]{1,0:T(8,128)(2,1)} %param.13) | copy-start | bytes 1920004
  352.5 4.4 %copy-start.5 = (f32[1600]{0:T(1024)S(1)}, f32[1600]{0:T(1024)}, u32[]{:S(2)}) copy-start(f32[1600]{0:T(1024)} %param.16) | copy-start | bytes 19204
Sparse Core Ops, SparseCore 0:
  15.1 50.1 reduce-scatter.3
  69.3 149.1 all-reduce.2
  220.3 65.6 all-gather.5
  355.9 39.6 all-gather.3

commit v3 on v2

--- a/solution.py
+++ b/solution.py
@@ -11,6 +11,7 @@
     layer_inputs, cotangents, weight, error_state, momentum, bias_momentum, start_basis, next_inputs
 ):
     highest = lax.Precision.HIGHEST
+    high = lax.Precision.HIGH
     group_count = lax.axis_size("grp")
     shard_count = lax.axis_size("shard")
     gradient = lax.psum_scatter(
@@ -24,20 +25,21 @@
     column_sums = jnp.sum(cotangents, axis=0, dtype=jnp.float32)
     corrected = gradient + error_state[0]
     own_rows = corrected.shape[0]
-    block = own_rows + 1
-    summed = lax.psum(jnp.concatenate([corrected, column_sums[None, :]], axis=0), "grp")
+    block = own_rows + 8
+    padding = jnp.zeros((block - own_rows - 1, corrected.shape[1]), jnp.float32)
+    summed = lax.psum(jnp.concatenate([corrected, column_sums[None, :], padding], axis=0), "grp")
     extended = lax.all_gather(summed, "shard", axis=0, tiled=True)
     all_sums = jnp.sum(extended.reshape(shard_count, block, -1)[:, own_rows], axis=0)
     is_total_row = (jnp.arange(shard_count * block) % block < own_rows)[:, None]
     basis = start_basis
     ortho = start_basis
     for round_index in range(2):
-        factor = jnp.where(is_total_row, jnp.dot(extended, basis, precision=highest), 0.0)
+        factor = jnp.where(is_total_row, jnp.dot(extended, basis, precision=high), 0.0)
         gram = jnp.dot(factor.T, factor, precision=highest)
         lower_factor = jnp.linalg.cholesky(gram)
         ortho = jax.scipy.linalg.solve_triangular(lower_factor, factor.T, lower=True).T
         basis = (
-            lax.dot_general(extended, ortho, (((0,), (0,)), ((), ())), precision=highest)
+            lax.dot_general(extended, ortho, (((0,), (0,)), ((), ())), precision=high)
             / group_count
         )
     own_ortho = lax.dynamic_slice_in_dim(ortho, lax.axis_index("shard") * block, own_rows, axis=0)

time: 410 us -> 398 us (0.971)
  local copies, waits for them, and re-layouts: 10.9 us -> 3 us
    unnamed x13 -> x18, local copies, waits for them, and re-layouts: 10.8 us -> 2.77 us
where the time goes in v3:
time: 398 us
  waiting for transfers between devices  304 us (76%)
  matrix products  58.2 us (15%)
  other arithmetic  18.2 us (5%)
  between operations  14 us (4%)
    psum x1, waiting for transfers between devices, shards(): lax.psum(jnp.concatenate([corrected, column_sums[None, :], padding], axis...  150 us
    all_gather x1, waiting for transfers between devices, shards(): extended = lax.all_gather(summed, 'shard', axis=0, tiled=True)  67.5 us
    unnamed x5, waiting for transfers between devices  48.6 us
    all_gather x1, waiting for transfers between devices, shards(): lax.all_gather(new_weight, 'shard', axis=0, tiled=True)  38.2 us
    dot_general x2, matrix products, shards(): lax.dot_general(extended, ortho, (((0,), (0,)), ((), ())), precision=high)  26 us
    dot_general x2, matrix products, shards(): jnp.dot(extended, basis, precision=high)  13.7 us
  transfers between devices with their start and end apart: 4, of which 4 were waited for; matrix products, arithmetic and copies ran while one was open for 1% of the time, Pallas kernels for 0%

profile of v3, /device:TPU:1, one launch (start us, length us, event | category | flops | bytes accessed | tf_op | source)
XLA Modules:
  0.0 398.0 jit_solution(11508757940438529201)
XLA Ops:
  7.2 0.0 copy-start
  7.2 0.0 reduce-scatter.4.cloned.1.call-start
  7.2 1.4 copy-done
  8.6 6.3 %convolution_convert_fusion = bf16[1600,1600]{1,0:T(8,128)(2,1)} fusion(bf16[512,1600]{0,1:T(8,128)(2,1)S(1)} %copy-done, bf16[512,1600]{0,1:T(8,128)(2,1)} %param.12), kind=kOutput, calls=%fused_computation | convolution fusion | flops 2624000000 | bytes 8396800 | tf_op jit(solution)/shard_map/dot_general | solution.py:18
  14.9 0.0 reduce-scatter.4.cloned.1.call-update
  15.0 0.0 all-reduce.3.cloned.1.call-start
  15.0 1.4 copy-done.1
  16.4 0.3 convert_reduce_fusion
  16.7 0.1 pad.2.clone
  16.8 48.5 %reduce-scatter.4.cloned.1.call-done = bf16[200,1600]{1,0:T(8,128)(2,1)} async-done(((bf16[1600,1600]{1,0:T(8,128)(2,1)}), bf16[200,1600]{1,0:T(8,128)(2,1)}) %reduce-scatter.4.cloned.1.call-update) | async-done | bytes 640016
  65.3 1.6 bitcast_add_fusion
  66.9 1.2 maximum_maximum_fusion
  68.2 0.0 all-reduce.3.cloned.1.call-update
  68.2 0.0 all-gather.3.cloned.1.call-start
  68.2 150.2 %all-reduce.3.cloned.1.call-done = f32[208,1600]{1,0:T(8,128)} async-done(((f32[208,1600]{1,0:T(8,128)}), f32[208,1600]{1,0:T(8,128)}) %all-reduce.3.cloned.1.call-update) | async-done | bytes 1331216 | tf_op jit(solution)/shard_map/psum | solution.py:30
  218.5 0.0 all-gather.3.cloned.1.call-update
  218.5 0.0 all-gather.5.cloned.1.call-start
  218.5 67.5 %all-gather.3.cloned.1.call-done = f32[1664,1600]{1,0:T(8,128)} async-done(((f32[208,1600]{1,0:T(8,128)}), f32[1664,1600]{1,0:T(8,128)}) %all-gather.3.cloned.1.call-update) | async-done | bytes 10649616 | tf_op jit(solution)/shard_map/all_gather | solution.py:31
  286.0 8.8 %convolution_select_fusion.1 = f32[1664,32]{0,1:T(8,128)S(1)} fusion(f32[1664,1600]{1,0:T(8,128)} %all-gather.3.cloned.1.call-done, f32[1600,32]{0,1:T(8,128)S(1)} %copy-done.4, pred[1664]{0:T(1024)(128)(4,1)S(1)} %fusion.15), kind=kOutput, calls=%fused_computation.7 | convolution fusion | flops 511234048 | bytes 11069056 | tf_op jit(solution)/shard_map/dot_general | solution.py:37
  294.9 0.3 fusion.22
  295.2 0.1 copy.14
  295.3 2.9 cholesky.44
  298.3 0.6 compare_reduce_fusion.1
  298.9 0.7 fusion.7
  299.6 2.4 custom-call.6
  302.0 0.4 fusion.3
  302.4 0.0 slice-start.1
  302.4 0.0 slice-start.2
  302.4 13.1 %convolution_multiply_fusion.1 = f32[1600,32]{1,0:T(8,128)S(1)} fusion(f32[1664,1600]{1,0:T(8,128)} %all-gather.3.cloned.1.call-done, f32[32,1664]{1,0:T(8,128)S(1)} %fusion.3), kind=kOutput, calls=%fused_computation.5 | convolution fusion | flops 511232000 | bytes 11067392 | tf_op jit(solution)/shard_map/dot_general | solution.py:42
  315.5 0.0 slice-done
  315.5 4.8 %convolution_select_fusion = f32[1664,32]{0,1:T(8,128)S(1)} fusion(f32[1664,1600]{1,0:T(8,128)S(1)} %bitcast.51, f32[1600,32]{1,0:T(8,128)S(1)} %convolution_multiply_fusion.1, pred[1664]{0:T(1024)(128)(4,1)S(1)} %fusion.15), kind=kOutput, calls=%fused_computation.6 | convolution fusion | flops 511234048 | bytes 11069056 | tf_op jit(solution)/shard_map/dot_general | solution.py:37
  320.4 0.3 fusion.23
  320.7 0.1 copy.15
  320.8 2.9 cholesky.55
  323.7 0.6 compare_reduce_fusion
  324.4 0.7 fusion.8
  325.0 2.4 custom-call.7
  327.5 0.4 fusion.1
  327.9 0.0 copy-start.2
  327.9 0.0 copy-start.3
  327.9 12.9 %convolution_multiply_fusion = f32[1600,32]{1,0:T(8,128)S(1)} fusion(f32[1664,1600]{1,0:T(8,128)} %all-gather.3.cloned.1.call-done, f32[32,1664]{1,0:T(8,128)S(1)} %fusion.1), kind=kOutput, calls=%fused_computation.4 | convolution fusion | flops 511232000 | bytes 11067392 | tf_op jit(solution)/shard_map/dot_general | solution.py:42
  340.9 0.0 copy-start.5
  340.9 3.4 subtract_convert_fusion
  344.3 0.0 all-gather.5.cloned.1.call-update
  344.3 1.0 slice_reduce_fusion
  345.4 0.6 multiply_add_fusion.1
  346.0 38.2 %all-gather.5.cloned.1.call-done = bf16[1600,1600]{1,0:T(8,128)(2,1)} async-done(((bf16[200,1600]{1,0:T(8,128)(2,1)}), bf16[1600,1600]{1,0:T(8,128)(2,1)}) %all-gather.5.cloned.1.call-update) | async-done | bytes 5120016 | tf_op jit(solution)/shard_map/all_gather | solution.py:53
  384.1 7.4 %fusion = bf16[512,1600]{0,1:T(8,128)(2,1)} fusion(bf16[1600,1600]{1,0:T(8,128)(2,1)} %all-gather.5.cloned.1.call-done, bf16[512,1600]{0,1:T(8,128)(2,1)} %param.18), kind=kOutput, calls=%fused_computation.3 | convolution fusion | flops 2622259200 | bytes 8396800 | tf_op jit(solution)/shard_map/dot_general | solution.py:51
  (17 shorter events, 0.1 us)
Async XLA Ops:
  7.2 1.4 copy-start
  7.2 58.1 %reduce-scatter.4.cloned.1.call-start = ((), (), s32[]{:S(2)}) async-start(), calls=%async_computation.4 | async-start | bytes 5990400
  14.9 1.4 copy-start.1
  15.0 203.5 %all-reduce.3.cloned.1.call-start = ((), (), s32[]{:S(2)}) async-start(), calls=%async_computation.1 | async-start | bytes 2768896 | tf_op jit(solution)/shard_map/psum | solution.py:30
  68.2 217.9 %copy-start.4 = (f32[1600,32]{0,1:T(8,128)S(1)}, f32[1600,32]{0,1:T(8,128)}, u32[]{:S(2)}) copy-start(f32[1600,32]{0,1:T(8,128)} %param.17) | copy-start | bytes 614404
  68.2 217.9 %all-gather.3.cloned.1.call-start = ((), (), s32[]{:S(2)}) async-start(), calls=%async_computation.2 | async-start | bytes 12460032 | tf_op jit(solution)/shard_map/all_gather | solution.py:31
  218.5 165.7 %all-gather.5.cloned.1.call-start = ((), (), s32[]{:S(2)}) async-start(), calls=%async_computation.3 | async-start | bytes 5990400 | tf_op jit(solution)/shard_map/all_gather | solution.py:53
  302.0 13.5 %slice-start = ((s8[11075584]{0:T(1024)(128)(4,1)}), s8[4194304]{0:T(1024)(128)(4,1)S(1)}, s32[]{:S(2)}) async-start(s8[11075584]{0:T(1024)(128)(4,1)} %bitcast.50), calls=%async_computation.5 | async-start | bytes 8388608
  302.4 13.1 %slice-start.1 = ((s8[11075584]{0:T(1024)(128)(4,1)}), s8[4194304]{0:T(1024)(128)(4,1)S(1)}, s32[]{:S(2)}) async-start(s8[11075584]{0:T(1024)(128)(4,1)} %bitcast.50), calls=%async_computation.6 | async-start | bytes 8388608
  302.4 13.1 %slice-start.2 = ((s8[11075584]{0:T(1024)(128)(4,1)}), s8[2686976]{0:T(1024)(128)(4,1)S(1)}, s32[]{:S(2)}) async-start(s8[11075584]{0:T(1024)(128)(4,1)} %bitcast.50), calls=%async_computation.7 | async-start | bytes 5373952
  327.9 13.0 %copy-start.2 = (f32[200,1600]{1,0:T(8,128)S(1)}, f32[200,1600]{1,0:T(8,128)}, u32[]{:S(2)}) copy-start(f32[200,1600]{1,0:T(8,128)} %param.15) | copy-start | bytes 3840004
  327.9 13.0 %copy-start.3 = (bf16[200,1600]{1,0:T(8,128)(2,1)S(1)}, bf16[200,1600]{1,0:T(8,128)(2,1)}, u32[]{:S(2)}) copy-start(bf16[200,1600]{1,0:T(8,128)(2,1)} %param.13) | copy-start | bytes 1920004
  340.9 4.5 %copy-start.5 = (f32[1600]{0:T(1024)S(1)}, f32[1600]{0:T(1024)}, u32[]{:S(2)}) copy-start(f32[1600]{0:T(1024)} %param.16) | copy-start | bytes 19204
Sparse Core Ops, SparseCore 0:
  15.1 50.1 reduce-scatter.3
  69.4 149.0 all-reduce.2
  220.3 65.6 all-gather.2
  344.4 39.6 all-gather.4

commit v4 on v3

--- a/solution.py
+++ b/solution.py
@@ -1,7 +1,7 @@
 import jax
 import jax.numpy as jnp
 from jax import lax
-from jax.sharding import PartitionSpec as P
+from jax.sharding import Mesh, PartitionSpec as P
 
 momentum_decay = 0.9
 learn_rate = 0.1
@@ -12,7 +12,7 @@
 ):
     highest = lax.Precision.HIGHEST
     high = lax.Precision.HIGH
-    group_count = lax.axis_size("grp")
+    group_count = lax.axis_size("gx") * lax.axis_size("gz")
     shard_count = lax.axis_size("shard")
     gradient = lax.psum_scatter(
         lax.dot_general(
@@ -27,7 +27,9 @@
     own_rows = corrected.shape[0]
     block = own_rows + 8
     padding = jnp.zeros((block - own_rows - 1, corrected.shape[1]), jnp.float32)
-    summed = lax.psum(jnp.concatenate([corrected, column_sums[None, :], padding], axis=0), "grp")
+    summed = lax.psum(
+        lax.psum(jnp.concatenate([corrected, column_sums[None, :], padding], axis=0), "gz"), "gx"
+    )
     extended = lax.all_gather(summed, "shard", axis=0, tiled=True)
     all_sums = jnp.sum(extended.reshape(shard_count, block, -1)[:, own_rows], axis=0)
     is_total_row = (jnp.arange(shard_count * block) % block < own_rows)[:, None]
@@ -56,21 +58,29 @@
     return (projected.astype(jnp.bfloat16), new_error, new_momentum, new_bias_momentum)
 
 
+def split_grp(mesh):
+    devices = mesh.devices
+    x_count = len({device.coords[0] for device in devices[:, 0]})
+    shape = (x_count, devices.shape[0] // x_count, devices.shape[1])
+    return Mesh(devices.reshape(shape), ("gx", "gz", "shard"))
+
+
 def solution(mesh):
+    grp = ("gx", "gz")
     placed = (
-        P(("grp", "shard"), None),
-        P(("grp", "shard"), None),
+        P((*grp, "shard"), None),
+        P((*grp, "shard"), None),
         P("shard", None),
-        P("grp", "shard", None),
+        P(grp, "shard", None),
         P("shard", None),
         P(),
         P(),
-        P(("grp", "shard"), None),
+        P((*grp, "shard"), None),
     )
     return jax.shard_map(
         shards,
-        mesh=mesh,
+        mesh=split_grp(mesh),
         in_specs=placed,
-        out_specs=(P(("grp", "shard"), None), P("grp", "shard", None), P("shard", None), P()),
+        out_specs=(P((*grp, "shard"), None), P(grp, "shard", None), P("shard", None), P()),
         check_vma=False,
     )

time: 398 us -> 381 us (0.957)
  waiting for transfers between devices: 304 us -> 288 us
    psum x1, waiting for transfers between devices: 150 us -> 75.7 us  [shards(): lax.psum(jnp.concatenate([corrected, column_sums[None, :], padding], axis...]
    psum x0 -> x1, waiting for transfers between devices: none -> 57.9 us  [shards(): lax.psum(lax.psum(jnp.concatenate([corrected, column_sums[None, :], paddi...]
    unnamed x5 -> x6, waiting for transfers between devices: 48.6 us -> 48.6 us
  transfers between devices with their start and end apart: 4 -> 5, of which waited for: 4 -> 5; matrix products, arithmetic and copies ran while one was open for 1% -> 1% of each run, Pallas kernels for 0% -> 0%
where the time goes in v4:
time: 381 us
  waiting for transfers between devices  288 us (76%)
  matrix products  58.2 us (15%)
  other arithmetic  18.2 us (5%)
  between operations  14 us (4%)
    psum x1, waiting for transfers between devices, shards(): lax.psum(jnp.concatenate([corrected, column_sums[None, :], padding], axis...  75.7 us
    all_gather x1, waiting for transfers between devices, shards(): extended = lax.all_gather(summed, 'shard', axis=0, tiled=True)  67.3 us
    psum x1, waiting for transfers between devices, shards(): lax.psum(lax.psum(jnp.concatenate([corrected, column_sums[None, :], paddi...  57.9 us
    unnamed x6, waiting for transfers between devices  48.6 us
    all_gather x1, waiting for transfers between devices, shards(): lax.all_gather(new_weight, 'shard', axis=0, tiled=True)  38.2 us
    dot_general x2, matrix products, shards(): lax.dot_general(extended, ortho, (((0,), (0,)), ((), ())), precision=high)  26 us
    dot_general x2, matrix products, shards(): jnp.dot(extended, basis, precision=high)  13.7 us
  transfers between devices with their start and end apart: 5, of which 5 were waited for; matrix products, arithmetic and copies ran while one was open for 1% of the time, Pallas kernels for 0%

profile of v4, /device:TPU:1, one launch (start us, length us, event | category | flops | bytes accessed | tf_op | source)
XLA Modules:
  0.0 381.2 jit_solution(10117569209977364248)
XLA Ops:
  7.2 0.0 copy-start
  7.2 0.0 reduce-scatter.4.cloned.1.call-start
  7.2 1.4 copy-done
  8.6 6.3 %convolution_convert_fusion = bf16[1600,1600]{1,0:T(8,128)(2,1)} fusion(bf16[512,1600]{0,1:T(8,128)(2,1)S(1)} %copy-done, bf16[512,1600]{0,1:T(8,128)(2,1)} %param.12), kind=kOutput, calls=%fused_computation | convolution fusion | flops 2624000000 | bytes 8396800 | tf_op jit(solution)/shard_map/dot_general | solution.py:18
  14.9 0.0 reduce-scatter.4.cloned.1.call-update
  15.0 0.0 all-reduce.4.cloned.1.call-start
  15.0 1.4 copy-done.1
  16.4 0.3 convert_reduce_fusion
  16.7 0.1 pad.2.clone
  16.8 48.5 %reduce-scatter.4.cloned.1.call-done = bf16[200,1600]{1,0:T(8,128)(2,1)} async-done(((bf16[1600,1600]{1,0:T(8,128)(2,1)}), bf16[200,1600]{1,0:T(8,128)(2,1)}) %reduce-scatter.4.cloned.1.call-update) | async-done | bytes 640016
  65.3 1.6 bitcast_add_fusion
  66.9 1.2 maximum_maximum_fusion
  68.2 0.0 all-reduce.4.cloned.1.call-update
  68.2 0.0 copy-start.4
  68.2 0.0 all-reduce.6.cloned.1.call-start
  68.2 75.7 %all-reduce.4.cloned.1.call-done = f32[208,1600]{1,0:T(8,128)} async-done(((f32[208,1600]{1,0:T(8,128)}), f32[208,1600]{1,0:T(8,128)}) %all-reduce.4.cloned.1.call-update) | async-done | bytes 1331216 | tf_op jit(solution)/shard_map/psum | solution.py:31
  143.9 0.0 all-reduce.6.cloned.1.call-update
  143.9 0.0 all-gather.3.cloned.1.call-start
  144.0 57.9 %all-reduce.6.cloned.1.call-done = f32[208,1600]{1,0:T(8,128)} async-done(((f32[208,1600]{1,0:T(8,128)}), f32[208,1600]{1,0:T(8,128)}) %all-reduce.6.cloned.1.call-update) | async-done | bytes 1331216 | tf_op jit(solution)/shard_map/psum | solution.py:30
  201.8 0.0 all-gather.3.cloned.1.call-update
  201.9 0.0 all-gather.5.cloned.1.call-start
  201.9 67.3 %all-gather.3.cloned.1.call-done = f32[1664,1600]{1,0:T(8,128)} async-done(((f32[208,1600]{1,0:T(8,128)}), f32[1664,1600]{1,0:T(8,128)}) %all-gather.3.cloned.1.call-update) | async-done | bytes 10649616 | tf_op jit(solution)/shard_map/all_gather | solution.py:33
  269.2 8.8 %convolution_select_fusion.1 = f32[1664,32]{0,1:T(8,128)S(1)} fusion(f32[1664,1600]{1,0:T(8,128)} %all-gather.3.cloned.1.call-done, f32[1600,32]{0,1:T(8,128)S(1)} %copy-done.4, pred[1664]{0:T(1024)(128)(4,1)S(1)} %fusion.15), kind=kOutput, calls=%fused_computation.7 | convolution fusion | flops 511234048 | bytes 11069056 | tf_op jit(solution)/shard_map/dot_general | solution.py:39
  278.0 0.3 fusion.22
  278.4 0.1 copy.14
  278.5 2.9 cholesky.44
  281.4 0.6 compare_reduce_fusion.1
  282.1 0.7 fusion.7
  282.7 2.4 custom-call.6
  285.1 0.4 fusion.3
  285.6 13.1 %convolution_multiply_fusion.1 = f32[1600,32]{1,0:T(8,128)S(1)} fusion(f32[1664,1600]{1,0:T(8,128)} %all-gather.3.cloned.1.call-done, f32[32,1664]{1,0:T(8,128)S(1)} %fusion.3), kind=kOutput, calls=%fused_computation.5 | convolution fusion | flops 511232000 | bytes 11067392 | tf_op jit(solution)/shard_map/dot_general | solution.py:44
  298.7 4.8 %convolution_select_fusion = f32[1664,32]{0,1:T(8,128)S(1)} fusion(f32[1664,1600]{1,0:T(8,128)S(1)} %bitcast.51, f32[1600,32]{1,0:T(8,128)S(1)} %convolution_multiply_fusion.1, pred[1664]{0:T(1024)(128)(4,1)S(1)} %fusion.15), kind=kOutput, calls=%fused_computation.6 | convolution fusion | flops 511234048 | bytes 11069056 | tf_op jit(solution)/shard_map/dot_general | solution.py:39
  303.5 0.3 fusion.23
  303.8 0.1 copy.15
  303.9 2.9 cholesky.55
  306.9 0.6 compare_reduce_fusion
  307.5 0.7 fusion.8
  308.2 2.4 custom-call.7
  310.6 0.4 fusion.1
  311.0 0.0 copy-start.2
  311.1 12.9 %convolution_multiply_fusion = f32[1600,32]{1,0:T(8,128)S(1)} fusion(f32[1664,1600]{1,0:T(8,128)} %all-gather.3.cloned.1.call-done, f32[32,1664]{1,0:T(8,128)S(1)} %fusion.1), kind=kOutput, calls=%fused_computation.4 | convolution fusion | flops 511232000 | bytes 11067392 | tf_op jit(solution)/shard_map/dot_general | solution.py:44
  324.0 0.0 copy-start.5
  324.0 3.4 subtract_convert_fusion
  327.4 0.0 all-gather.5.cloned.1.call-update
  327.5 1.0 slice_reduce_fusion
  328.5 0.6 multiply_add_fusion.1
  329.1 38.2 %all-gather.5.cloned.1.call-done = bf16[1600,1600]{1,0:T(8,128)(2,1)} async-done(((bf16[200,1600]{1,0:T(8,128)(2,1)}), bf16[1600,1600]{1,0:T(8,128)(2,1)}) %all-gather.5.cloned.1.call-update) | async-done | bytes 5120016 | tf_op jit(solution)/shard_map/all_gather | solution.py:55
  367.3 7.4 %fusion = bf16[512,1600]{0,1:T(8,128)(2,1)} fusion(bf16[1600,1600]{1,0:T(8,128)(2,1)} %all-gather.5.cloned.1.call-done, bf16[512,1600]{0,1:T(8,128)(2,1)} %param.18), kind=kOutput, calls=%fused_computation.3 | convolution fusion | flops 2622259200 | bytes 8396800 | tf_op jit(solution)/shard_map/dot_general | solution.py:53
  (20 shorter events, 0.1 us)
Async XLA Ops:
  7.2 1.4 copy-start
  7.2 58.1 %reduce-scatter.4.cloned.1.call-start = ((), (), s32[]{:S(2)}) async-start(), calls=%async_computation.5 | async-start | bytes 5990400
  14.9 1.4 copy-start.1
  15.0 129.0 %all-reduce.4.cloned.1.call-start = ((), (), s32[]{:S(2)}) async-start(), calls=%async_computation.1 | async-start | bytes 2768896 | tf_op jit(solution)/shard_map/psum | solution.py:31
  68.2 201.0 %copy-start.4 = (f32[1600,32]{0,1:T(8,128)S(1)}, f32[1600,32]{0,1:T(8,128)}, u32[]{:S(2)}) copy-start(f32[1600,32]{0,1:T(8,128)} %param.17) | copy-start | bytes 614404
  68.2 133.7 %all-reduce.6.cloned.1.call-start = ((), (), s32[]{:S(2)}) async-start(), calls=%async_computation.2 | async-start | bytes 2768896 | tf_op jit(solution)/shard_map/psum | solution.py:30
  143.9 125.3 %all-gather.3.cloned.1.call-start = ((), (), s32[]{:S(2)}) async-start(), calls=%async_computation.3 | async-start | bytes 12460032 | tf_op jit(solution)/shard_map/all_gather | solution.py:33
  201.9 165.4 %all-gather.5.cloned.1.call-start = ((), (), s32[]{:S(2)}) async-start(), calls=%async_computation.4 | async-start | bytes 5990400 | tf_op jit(solution)/shard_map/all_gather | solution.py:55
  285.1 13.5 %slice-start = ((s8[11075584]{0:T(1024)(128)(4,1)}), s8[4194304]{0:T(1024)(128)(4,1)S(1)}, s32[]{:S(2)}) async-start(s8[11075584]{0:T(1024)(128)(4,1)} %bitcast.50), calls=%async_computation.6 | async-start | bytes 8388608
  285.6 13.1 %slice-start.1 = ((s8[11075584]{0:T(1024)(128)(4,1)}), s8[4194304]{0:T(1024)(128)(4,1)S(1)}, s32[]{:S(2)}) async-start(s8[11075584]{0:T(1024)(128)(4,1)} %bitcast.50), calls=%async_computation.7 | async-start | bytes 8388608
  285.6 13.1 %slice-start.2 = ((s8[11075584]{0:T(1024)(128)(4,1)}), s8[2686976]{0:T(1024)(128)(4,1)S(1)}, s32[]{:S(2)}) async-start(s8[11075584]{0:T(1024)(128)(4,1)} %bitcast.50), calls=%async_computation.8 | async-start | bytes 5373952
  311.0 13.0 %copy-start.2 = (f32[200,1600]{1,0:T(8,128)S(1)}, f32[200,1600]{1,0:T(8,128)}, u32[]{:S(2)}) copy-start(f32[200,1600]{1,0:T(8,128)} %param.15) | copy-start | bytes 3840004
  311.0 13.0 %copy-start.3 = (bf16[200,1600]{1,0:T(8,128)(2,1)S(1)}, bf16[200,1600]{1,0:T(8,128)(2,1)}, u32[]{:S(2)}) copy-start(bf16[200,1600]{1,0:T(8,128)(2,1)} %param.13) | copy-start | bytes 1920004
  324.0 4.5 %copy-start.5 = (f32[1600]{0:T(1024)S(1)}, f32[1600]{0:T(1024)}, u32[]{:S(2)}) copy-start(f32[1600]{0:T(1024)} %param.16) | copy-start | bytes 19204
Sparse Core Ops, SparseCore 0:
  15.1 50.1 reduce-scatter.3
  68.3 75.5 all-reduce.3
  146.3 55.4 all-reduce.5
  203.5 65.6 all-gather.2
  327.6 39.6 all-gather.4

commit v5 on v4

--- a/solution.py
+++ b/solution.py
@@ -11,7 +11,7 @@
     layer_inputs, cotangents, weight, error_state, momentum, bias_momentum, start_basis, next_inputs
 ):
     highest = lax.Precision.HIGHEST
-    high = lax.Precision.HIGH
+    rank = start_basis.shape[1]
     group_count = lax.axis_size("gx") * lax.axis_size("gz")
     shard_count = lax.axis_size("shard")
     gradient = lax.psum_scatter(
@@ -30,20 +30,44 @@
     summed = lax.psum(
         lax.psum(jnp.concatenate([corrected, column_sums[None, :], padding], axis=0), "gz"), "gx"
     )
-    extended = lax.all_gather(summed, "shard", axis=0, tiled=True)
-    all_sums = jnp.sum(extended.reshape(shard_count, block, -1)[:, own_rows], axis=0)
+    high_part = summed.astype(jnp.bfloat16)
+    low_part = (summed - high_part.astype(jnp.float32)).astype(jnp.bfloat16)
+    gathered = lax.all_gather(
+        jnp.concatenate([high_part, low_part], axis=0), "shard", axis=0, tiled=True
+    )
+    split_rows = gathered.reshape(shard_count, 2, block, -1)
+    sum_rows = split_rows[:, :, own_rows].astype(jnp.float32)
+    all_sums = jnp.sum(sum_rows[:, 0] + sum_rows[:, 1], axis=0)
     is_total_row = (jnp.arange(shard_count * block) % block < own_rows)[:, None]
+
+    def pair(values):
+        upper = values.astype(jnp.bfloat16)
+        return upper, (values - upper.astype(jnp.float32)).astype(jnp.bfloat16)
+
     basis = start_basis
     ortho = start_basis
     for round_index in range(2):
-        factor = jnp.where(is_total_row, jnp.dot(extended, basis, precision=high), 0.0)
+        basis_high, basis_low = pair(basis)
+        both = jnp.dot(
+            gathered, jnp.concatenate([basis_high, basis_low], axis=1), preferred_element_type=jnp.float32
+        ).reshape(shard_count, 2, block, 2 * rank)
+        product = both[:, 0, :, :rank] + both[:, 0, :, rank:] + both[:, 1, :, :rank]
+        factor = jnp.where(is_total_row, product.reshape(shard_count * block, rank), 0.0)
         gram = jnp.dot(factor.T, factor, precision=highest)
         lower_factor = jnp.linalg.cholesky(gram)
         ortho = jax.scipy.linalg.solve_triangular(lower_factor, factor.T, lower=True).T
-        basis = (
-            lax.dot_general(extended, ortho, (((0,), (0,)), ((), ())), precision=high)
-            / group_count
+        ortho_high, ortho_low = pair(ortho.reshape(shard_count, 1, block, rank))
+        weights = jnp.concatenate(
+            [
+                jnp.concatenate([ortho_high, ortho_high], axis=1),
+                jnp.concatenate([ortho_low, jnp.zeros_like(ortho_low)], axis=1),
+            ],
+            axis=3,
+        ).reshape(shard_count * 2 * block, 2 * rank)
+        terms = lax.dot_general(
+            gathered, weights, (((0,), (0,)), ((), ())), preferred_element_type=jnp.float32
         )
+        basis = (terms[:, :rank] + terms[:, rank:]) / group_count
     own_ortho = lax.dynamic_slice_in_dim(ortho, lax.axis_index("shard") * block, own_rows, axis=0)
     approx = jnp.dot(own_ortho, basis.T, precision=highest)
     new_error = (corrected - approx)[None, :, :]

time: 381 us -> 399 us (1.047)
  local copies, waits for them, and re-layouts: 3 us -> 21.9 us
  matrix products: 58.2 us -> 50.1 us
  other arithmetic: 18.2 us -> 25.6 us
    reshape x0 -> x6, local copies, waits for them, and re-layouts: none -> 13.4 us  [the longest x2 7.73 us: shards(): both = jnp.dot(gathered, jnp.concatenate([basis_high, basis_low], axis=1)...]
    dot_general x4, matrix products: 39.6 us -> 29.1 us  [the longest x2 16.6 us: shards(): jnp.dot(gathered, jnp.concatenate([basis_high, basis_low], axis=1), prefe...]
    concatenate x0 -> x3, other arithmetic: none -> 4.65 us  [the longest x2 3.46 us: shards(): jnp.concatenate([jnp.concatenate([ortho_high, ortho_high], axis=1), jnp.c...]
    slice x0 -> x2, local copies, waits for them, and re-layouts: none -> 4.44 us  [shards(): product = both[:, 0, :, :rank] + both[:, 0, :, rank:] + both[:, 1, :, :rank]]
where the time goes in v5:
time: 399 us; the launch traced here: 398 us
  waiting for transfers between devices  286 us (72%)
  matrix products  50.1 us (13%)
  other arithmetic  25.6 us (6%)
  local copies, waits for them, and re-layouts  21.9 us (5%)
  between operations  14.1 us (4%)
    psum x1, waiting for transfers between devices, shards(): lax.psum(jnp.concatenate([corrected, column_sums[None, :], padding], axis...  75.7 us
    all_gather x1, waiting for transfers between devices, shards(): lax.all_gather(jnp.concatenate([high_part, low_part], axis=0), 'shard', a...  65.5 us
    psum x1, waiting for transfers between devices, shards(): lax.psum(lax.psum(jnp.concatenate([corrected, column_sums[None, :], paddi...  57.9 us
    unnamed x6, waiting for transfers between devices  48.6 us
    all_gather x1, waiting for transfers between devices, shards(): lax.all_gather(new_weight, 'shard', axis=0, tiled=True)  38 us
    dot_general x2, matrix products, shards(): jnp.dot(gathered, jnp.concatenate([basis_high, basis_low], axis=1), prefe...  16.6 us
    dot_general x2, matrix products, shards(): lax.dot_general(gathered, weights, (((0,), (0,)), ((), ())), preferred_el...  12.5 us
  transfers between devices with their start and end apart: 5, of which 5 were waited for; matrix products, arithmetic and copies ran while one was open for 1% of the time, Pallas kernels for 0%

profile of v5, /device:TPU:1, one launch (start us, length us, event | category | flops | bytes accessed | tf_op | source)
XLA Modules:
  0.0 397.8 jit_solution(5483412051702157521)
XLA Ops:
  7.2 1.4 copy-done
  8.6 6.3 %convolution_convert_fusion = bf16[1600,1600]{1,0:T(8,128)(2,1)} fusion(bf16[512,1600]{0,1:T(8,128)(2,1)S(1)} %copy-done, bf16[512,1600]{0,1:T(8,128)(2,1)} %param.12), kind=kOutput, calls=%fused_computation | convolution fusion | flops 2624000000 | bytes 8396800 | tf_op jit(solution)/shard_map/dot_general | solution.py:18
  15.0 1.4 copy-done.1
  16.4 0.3 convert_reduce_fusion
  16.8 48.5 %reduce-scatter.4.cloned.1.call-done = bf16[200,1600]{1,0:T(8,128)(2,1)} async-done(((bf16[1600,1600]{1,0:T(8,128)(2,1)}), bf16[200,1600]{1,0:T(8,128)(2,1)}) %reduce-scatter.4.cloned.1.call-update) | async-done | bytes 640016
  65.3 1.6 bitcast_add_fusion
  66.9 1.2 maximum_maximum_fusion
  68.2 75.7 %all-reduce.6.cloned.1.call-done = f32[208,1600]{1,0:T(8,128)} async-done(((f32[208,1600]{1,0:T(8,128)}), f32[208,1600]{1,0:T(8,128)}) %all-reduce.6.cloned.1.call-update) | async-done | bytes 1331216 | tf_op jit(solution)/shard_map/psum | solution.py:31
  144.0 57.9 %all-reduce.8.cloned.1.call-done = f32[208,1600]{1,0:T(8,128)} async-done(((f32[208,1600]{1,0:T(8,128)}), f32[208,1600]{1,0:T(8,128)}) %all-reduce.8.cloned.1.call-update) | async-done | bytes 1331216 | tf_op jit(solution)/shard_map/psum | solution.py:30
  201.8 1.9 subtract_convert_fusion
  203.8 1.2 pad_maximum_fusion
  205.0 0.2 all-gather.5.cloned.1.call-start
  205.3 65.5 %all-gather.3.cloned.1.call-done = bf16[3328,1600]{1,0:T(8,128)(2,1)} async-done(((bf16[416,1600]{1,0:T(8,128)(2,1)}), bf16[3328,1600]{1,0:T(8,128)(2,1)}) %all-gather.3.cloned.1.call-update) | async-done | bytes 10649616 | tf_op jit(solution)/shard_map/all_gather | solution.py:35
  270.8 8.3 %fusion.12 = f32[3328,64]{0,1:T(8,128)} fusion(bf16[3328,1600]{1,0:T(8,128)(2,1)} %all-gather.3.cloned.1.call-done, bf16[1600,32]{0,1:T(8,128)(2,1)S(1)} %get-tuple-element.14, bf16[1600,32]{0,1:T(8,128)(2,1)S(1)} %get-tuple-element.15), kind=kOutput, calls=%fused_computation.35 | convolution fusion | flops 681984000 | bytes 11706368 | tf_op jit(solution)/shard_map/dot_general | solution.py:51
  279.1 3.9 reshape.175
  282.9 2.1 fusion.57
  285.1 0.4 convolution_bitcast_fusion.2
  285.6 2.9 cholesky.44
  288.6 0.6 compare_reduce_fusion.1
  289.2 0.7 fusion.33
  289.9 2.4 custom-call.6
  292.3 0.2 add.96
  292.5 1.1 convolution_bitcast_fusion
  293.5 1.5 reshape.188
  295.0 0.3 fusion.59
  295.3 1.7 fusion.3
  297.1 1.8 reshape.178
  298.9 6.2 %fusion.64 = f32[1600,64]{0,1:T(8,128)S(1)} fusion(bf16[3328,64]{0,1:T(8,128)(2,1)S(1)} %reshape.178, bf16[3328,1600]{1,0:T(8,128)(2,1)} %all-gather.3.cloned.1.call-done), kind=kOutput, calls=%fused_computation.101 | convolution fusion | flops 681574400 | bytes 11485184 | tf_op jit(solution)/shard_map/dot_general | solution.py:67
  305.1 8.3 %fusion.16 = f32[3328,64]{0,1:T(8,128)} fusion(bf16[3328,1600]{1,0:T(8,128)(2,1)} %all-gather.3.cloned.1.call-done, bf16[1600,32]{0,1:T(8,128)(2,1)S(1)} %get-tuple-element.10, bf16[1600,32]{0,1:T(8,128)(2,1)S(1)} %get-tuple-element.11), kind=kOutput, calls=%fused_computation.39 | convolution fusion | flops 681984000 | bytes 11706368 | tf_op jit(solution)/shard_map/dot_general | solution.py:51
  313.4 3.9 reshape.179
  317.3 2.3 fusion.56
  319.7 0.4 convolution_bitcast_fusion.1
  320.2 2.9 cholesky.55
  323.1 0.6 compare_reduce_fusion
  323.8 0.7 fusion.34
  324.4 2.4 custom-call.7
  326.8 0.9 add.100
  327.7 1.3 fusion.20
  329.0 0.6 reshape.189
  329.6 0.3 fusion.58
  329.9 1.7 fusion.4
  331.7 1.8 reshape.182
  333.5 6.3 %fusion.65 = f32[1600,64]{0,1:T(8,128)S(1)} fusion(bf16[3328,64]{0,1:T(8,128)(2,1)S(1)} %reshape.182, bf16[3328,1600]{1,0:T(8,128)(2,1)} %all-gather.3.cloned.1.call-done), kind=kOutput, calls=%fused_computation.102 | convolution fusion | flops 681574400 | bytes 11485184 | tf_op jit(solution)/shard_map/dot_general | solution.py:67
  339.9 4.2 %subtract_convert_fusion.1 = (bf16[200,1600]{1,0:T(8,128)(2,1)}, f32[200,1600]{1,0:T(8,128)}, f32[1,200,1600]{2,1,0:T(8,128)}) fusion(bf16[200,1600]{1,0:T(8,128)(2,1)S(1)} %copy-done.4, f32[200,1600]{1,0:T(8,128)S(1)} %copy-done.2, f32[200,1600]{1,0:T(8,128)S(1)} %bitcast_add_fusion, f32[1600,64]{0,1:T(8,128)S(1)} %fusion.65, f32[32,1664]{1,0:T(8,128)} %copy-done.3, ...), kind=kOutput, calls=%fused_computation.10 | convolution fusion | flops 125222400 | bytes 6842372 | tf_op jit(solution)/shard_map/dot_general | solution.py:72
  344.1 1.1 slice_convert_fusion
  345.3 0.6 multiply_add_fusion.1
  345.9 38.0 %all-gather.5.cloned.1.call-done = bf16[1600,1600]{1,0:T(8,128)(2,1)} async-done(((bf16[200,1600]{1,0:T(8,128)(2,1)}), bf16[1600,1600]{1,0:T(8,128)(2,1)}) %all-gather.5.cloned.1.call-update) | async-done | bytes 5120016 | tf_op jit(solution)/shard_map/all_gather | solution.py:79
  383.9 7.4 %fusion = bf16[512,1600]{0,1:T(8,128)(2,1)} fusion(bf16[1600,1600]{1,0:T(8,128)(2,1)} %all-gather.5.cloned.1.call-done, bf16[512,1600]{0,1:T(8,128)(2,1)} %param.18), kind=kOutput, calls=%fused_computation.3 | convolution fusion | flops 2622259200 | bytes 8396800 | tf_op jit(solution)/shard_map/dot_general | solution.py:77
  (38 shorter events, 0.9 us)
Async XLA Ops:
  7.2 1.4 copy-start
  7.2 58.1 %reduce-scatter.4.cloned.1.call-start = ((), (), s32[]{:S(2)}) async-start(), calls=%async_computation.5 | async-start | bytes 5990400
  14.9 1.4 copy-start.1
  15.0 129.0 %all-reduce.6.cloned.1.call-start = ((), (), s32[]{:S(2)}) async-start(), calls=%async_computation.1 | async-start | bytes 2768896 | tf_op jit(solution)/shard_map/psum | solution.py:31
  68.2 133.7 %all-reduce.8.cloned.1.call-start = ((), (), s32[]{:S(2)}) async-start(), calls=%async_computation.2 | async-start | bytes 2768896 | tf_op jit(solution)/shard_map/psum | solution.py:30
  143.9 126.8 %all-gather.3.cloned.1.call-start = ((), (), s32[]{:S(2)}) async-start(), calls=%async_computation.3 | async-start | bytes 12460032 | tf_op jit(solution)/shard_map/all_gather | solution.py:35
  203.8 1.5 copy-start.5
  205.0 178.9 %all-gather.5.cloned.1.call-start = ((), (), s32[]{:S(2)}) async-start(), calls=%async_computation.4 | async-start | bytes 5990400 | tf_op jit(solution)/shard_map/all_gather | solution.py:79
  329.0 0.9 copy-start.3
  333.5 6.4 %copy-start.2 = (f32[200,1600]{1,0:T(8,128)S(1)}, f32[200,1600]{1,0:T(8,128)}, u32[]{:S(2)}) copy-start(f32[200,1600]{1,0:T(8,128)} %param.15) | copy-start | bytes 3840004
  333.5 6.4 %copy-start.4 = (bf16[200,1600]{1,0:T(8,128)(2,1)S(1)}, bf16[200,1600]{1,0:T(8,128)(2,1)}, u32[]{:S(2)}) copy-start(bf16[200,1600]{1,0:T(8,128)(2,1)} %param.13) | copy-start | bytes 1920004
  339.9 5.4 %copy-start.6 = (f32[1600]{0:T(1024)S(1)}, f32[1600]{0:T(1024)}, u32[]{:S(2)}) copy-start(f32[1600]{0:T(1024)} %param.16) | copy-start | bytes 19204
Sparse Core Ops, SparseCore 0:
  15.1 50.1 reduce-scatter.3
  68.3 75.5 all-reduce.5
  146.3 55.4 all-reduce.7
  205.1 65.6 all-gather.2
  344.2 39.6 all-gather.4

commit v6 on v4

--- a/solution.py
+++ b/solution.py
@@ -25,12 +25,11 @@
     column_sums = jnp.sum(cotangents, axis=0, dtype=jnp.float32)
     corrected = gradient + error_state[0]
     own_rows = corrected.shape[0]
-    block = own_rows + 8
+    block = own_rows + 24
     padding = jnp.zeros((block - own_rows - 1, corrected.shape[1]), jnp.float32)
-    summed = lax.psum(
-        lax.psum(jnp.concatenate([corrected, column_sums[None, :], padding], axis=0), "gz"), "gx"
-    )
-    extended = lax.all_gather(summed, "shard", axis=0, tiled=True)
+    z_summed = lax.psum(jnp.concatenate([corrected, column_sums[None, :], padding], axis=0), "gz")
+    piece = lax.psum_scatter(z_summed, "gx", scatter_dimension=0, tiled=True)
+    extended = lax.all_gather(piece, ("shard", "gx"), axis=0, tiled=True)
     all_sums = jnp.sum(extended.reshape(shard_count, block, -1)[:, own_rows], axis=0)
     is_total_row = (jnp.arange(shard_count * block) % block < own_rows)[:, None]
     basis = start_basis

time: 381 us -> 355 us (0.932)
  waiting for transfers between devices: 288 us -> 259 us
    psum x1 -> x0, waiting for transfers between devices: 57.9 us -> none  [shards(): lax.psum(lax.psum(jnp.concatenate([corrected, column_sums[None, :], paddi...]
    unnamed x6 -> x7, waiting for transfers between devices: 48.6 us -> 77.6 us
    all_gather x1, waiting for transfers between devices: 67.3 us -> 72.6 us  [shards(): extended = lax.all_gather(piece, ('shard', 'gx'), axis=0, tiled=True)]
    psum x1, waiting for transfers between devices: 75.7 us -> 71.5 us  [shards(): lax.psum(jnp.concatenate([corrected, column_sums[None, :], padding], axis...]
where the time goes in v6:
time: 355 us
  waiting for transfers between devices  259 us (73%)
  matrix products  60.5 us (17%)
  other arithmetic  18.2 us (5%)
  between operations  14 us (4%)
    unnamed x7, waiting for transfers between devices  77.6 us
    all_gather x1, waiting for transfers between devices, shards(): extended = lax.all_gather(piece, ('shard', 'gx'), axis=0, tiled=True)  72.6 us
    psum x1, waiting for transfers between devices, shards(): lax.psum(jnp.concatenate([corrected, column_sums[None, :], padding], axis...  71.5 us
    all_gather x1, waiting for transfers between devices, shards(): lax.all_gather(new_weight, 'shard', axis=0, tiled=True)  37.5 us
    dot_general x2, matrix products, shards(): lax.dot_general(extended, ortho, (((0,), (0,)), ((), ())), precision=high)  27.4 us
    dot_general x2, matrix products, shards(): jnp.dot(extended, basis, precision=high)  14.6 us
    dot_general x1, matrix products, shards(): jnp.dot(next_inputs, lax.all_gather(new_weight, 'shard', axis=0, tiled=Tr...  7.35 us
    another operation x6, other arithmetic, shards(): lower_factor = jnp.linalg.cholesky(gram)  7.2 us
  transfers between devices with their start and end apart: 5, of which 5 were waited for; matrix products, arithmetic and copies ran while one was open for 1% of the time, Pallas kernels for 0%

profile of v6, /device:TPU:1, one launch (start us, length us, event | category | flops | bytes accessed | tf_op | source)
XLA Modules:
  0.0 355.1 jit_solution(13201662149218956643)
XLA Ops:
  7.2 0.0 copy-start
  7.2 0.0 reduce-scatter.7.cloned.1.call-start
  7.2 1.4 copy-done
  8.6 6.3 %convolution_convert_fusion = bf16[1600,1600]{1,0:T(8,128)(2,1)} fusion(bf16[512,1600]{0,1:T(8,128)(2,1)S(1)} %copy-done, bf16[512,1600]{0,1:T(8,128)(2,1)} %param.12), kind=kOutput, calls=%fused_computation | convolution fusion | flops 2624000000 | bytes 8396800 | tf_op jit(solution)/shard_map/dot_general | solution.py:18
  14.9 0.0 reduce-scatter.7.cloned.1.call-update
  15.0 0.0 reduce-scatter.9.cloned.1.call-start
  15.0 1.4 copy-done.1
  16.4 0.3 convert_reduce_fusion
  16.7 0.1 pad.2.clone
  16.8 48.5 %reduce-scatter.7.cloned.1.call-done = bf16[200,1600]{1,0:T(8,128)(2,1)} async-done(((bf16[1600,1600]{1,0:T(8,128)(2,1)}), bf16[200,1600]{1,0:T(8,128)(2,1)}) %reduce-scatter.7.cloned.1.call-update) | async-done | bytes 640016
  65.3 1.6 bitcast_add_fusion
  66.9 1.3 maximum_maximum_fusion
  68.2 0.0 reduce-scatter.9.cloned.1.call-update
  68.2 0.0 all-reduce.4.cloned.1.call-start
  68.3 28.9 %reduce-scatter.9.cloned.1.call-done = f32[56,1600]{1,0:T(8,128)} async-done(((f32[224,1600]{1,0:T(8,128)}), f32[56,1600]{1,0:T(8,128)}) %reduce-scatter.9.cloned.1.call-update) | async-done | bytes 358416
  97.2 0.0 all-reduce.4.cloned.1.call-update
  97.2 0.0 all-gather.3.cloned.1.call-start
  97.3 71.5 %all-reduce.4.cloned.1.call-done = f32[56,1600]{1,0:T(8,128)} async-done(((f32[56,1600]{1,0:T(8,128)}), f32[56,1600]{1,0:T(8,128)}) %all-reduce.4.cloned.1.call-update) | async-done | bytes 358416 | tf_op jit(solution)/shard_map/psum | solution.py:30
  168.7 0.0 all-gather.3.cloned.1.call-update
  168.8 0.0 all-gather.5.cloned.1.call-start
  168.8 72.6 %all-gather.3.cloned.1.call-done = f32[1792,1600]{1,0:T(8,128)} async-done(((f32[56,1600]{1,0:T(8,128)}), f32[1792,1600]{1,0:T(8,128)}) %all-gather.3.cloned.1.call-update) | async-done | bytes 11468816 | tf_op jit(solution)/shard_map/all_gather | solution.py:32
  241.4 9.2 %convolution_select_fusion = f32[1792,32]{0,1:T(8,128)S(1)} fusion(f32[1792,1600]{1,0:T(8,128)} %all-gather.3.cloned.1.call-done, f32[1600,32]{0,1:T(8,128)S(1)} %copy-done.4, pred[1792]{0:T(1024)(128)(4,1)S(1)} %fusion.15), kind=kOutput, calls=%fused_computation.6 | convolution fusion | flops 550559744 | bytes 11904768 | tf_op jit(solution)/shard_map/dot_general | solution.py:38
  250.6 0.3 fusion.22
  250.9 0.1 copy.14
  251.0 2.9 cholesky.44
  254.0 0.6 compare_reduce_fusion.1
  254.6 0.7 fusion.7
  255.3 2.4 custom-call.6
  257.7 0.4 fusion.3
  258.2 13.8 %convolution_multiply_fusion.1 = f32[1600,32]{1,0:T(8,128)S(1)} fusion(f32[1792,1600]{1,0:T(8,128)} %all-gather.3.cloned.1.call-done, f32[32,1792]{1,0:T(8,128)S(1)} %fusion.3), kind=kOutput, calls=%fused_computation.5 | convolution fusion | flops 550553600 | bytes 11902976 | tf_op jit(solution)/shard_map/dot_general | solution.py:43
  272.0 5.4 %convolution_select_fusion.1 = f32[1792,32]{0,1:T(8,128)S(1)} fusion(f32[1792,1600]{1,0:T(8,128)S(1)} %bitcast.52, f32[1600,32]{1,0:T(8,128)S(1)} %convolution_multiply_fusion.1, pred[1792]{0:T(1024)(128)(4,1)S(1)} %fusion.15), kind=kOutput, calls=%fused_computation.7 | convolution fusion | flops 550559744 | bytes 11904768 | tf_op jit(solution)/shard_map/dot_general | solution.py:38
  277.3 0.3 fusion.23
  277.6 0.1 copy.15
  277.8 2.9 cholesky.55
  280.7 0.6 compare_reduce_fusion
  281.4 0.7 fusion.8
  282.0 2.4 custom-call.7
  284.5 0.4 fusion.1
  284.9 0.0 copy-start.2
  284.9 0.0 copy-start.3
  284.9 13.7 %convolution_multiply_fusion = f32[1600,32]{1,0:T(8,128)S(1)} fusion(f32[1792,1600]{1,0:T(8,128)} %all-gather.3.cloned.1.call-done, f32[32,1792]{1,0:T(8,128)S(1)} %fusion.1), kind=kOutput, calls=%fused_computation.4 | convolution fusion | flops 550553600 | bytes 11902976 | tf_op jit(solution)/shard_map/dot_general | solution.py:43
  298.6 0.0 copy-start.5
  298.6 3.4 subtract_convert_fusion
  302.0 0.0 all-gather.5.cloned.1.call-update
  302.0 1.0 slice_reduce_fusion
  303.1 0.6 multiply_add_fusion.1
  303.7 37.5 %all-gather.5.cloned.1.call-done = bf16[1600,1600]{1,0:T(8,128)(2,1)} async-done(((bf16[200,1600]{1,0:T(8,128)(2,1)}), bf16[1600,1600]{1,0:T(8,128)(2,1)}) %all-gather.5.cloned.1.call-update) | async-done | bytes 5120016 | tf_op jit(solution)/shard_map/all_gather | solution.py:54
  341.2 7.4 %fusion = bf16[512,1600]{0,1:T(8,128)(2,1)} fusion(bf16[1600,1600]{1,0:T(8,128)(2,1)} %all-gather.5.cloned.1.call-done, bf16[512,1600]{0,1:T(8,128)(2,1)} %param.18), kind=kOutput, calls=%fused_computation.3 | convolution fusion | flops 2622259200 | bytes 8396800 | tf_op jit(solution)/shard_map/dot_general | solution.py:52
  (20 shorter events, 0.1 us)
Async XLA Ops:
  7.2 1.4 copy-start
  7.2 58.1 %reduce-scatter.7.cloned.1.call-start = ((), (), s32[]{:S(2)}) async-start(), calls=%async_computation.5 | async-start | bytes 5990400
  14.9 1.4 copy-start.1
  15.0 82.2 %reduce-scatter.9.cloned.1.call-start = ((), (), s32[]{:S(2)}) async-start(), calls=%async_computation.6 | async-start | bytes 1863680
  68.2 173.2 %copy-start.4 = (f32[1600,32]{0,1:T(8,128)S(1)}, f32[1600,32]{0,1:T(8,128)}, u32[]{:S(2)}) copy-start(f32[1600,32]{0,1:T(8,128)} %param.17) | copy-start | bytes 614404
  68.2 100.5 %all-reduce.4.cloned.1.call-start = ((), (), s32[]{:S(2)}) async-start(), calls=%async_computation.4 | async-start | bytes 745472 | tf_op jit(solution)/shard_map/psum | solution.py:30
  97.2 144.2 %all-gather.3.cloned.1.call-start = ((), (), s32[]{:S(2)}) async-start(), calls=%async_computation.2 | async-start | bytes 12300288 | tf_op jit(solution)/shard_map/all_gather | solution.py:32
  168.8 172.4 %all-gather.5.cloned.1.call-start = ((), (), s32[]{:S(2)}) async-start(), calls=%async_computation.3 | async-start | bytes 5990400 | tf_op jit(solution)/shard_map/all_gather | solution.py:54
  257.7 14.2 %slice-start = ((s8[11927552]{0:T(1024)(128)(4,1)}), s8[4194304]{0:T(1024)(128)(4,1)S(1)}, s32[]{:S(2)}) async-start(s8[11927552]{0:T(1024)(128)(4,1)} %bitcast.51), calls=%async_computation.7 | async-start | bytes 8388608
  258.2 13.8 %slice-start.1 = ((s8[11927552]{0:T(1024)(128)(4,1)}), s8[4194304]{0:T(1024)(128)(4,1)S(1)}, s32[]{:S(2)}) async-start(s8[11927552]{0:T(1024)(128)(4,1)} %bitcast.51), calls=%async_computation.8 | async-start | bytes 8388608
  258.2 13.8 %slice-start.2 = ((s8[11927552]{0:T(1024)(128)(4,1)}), s8[3538944]{0:T(1024)(128)(4,1)S(1)}, s32[]{:S(2)}) async-start(s8[11927552]{0:T(1024)(128)(4,1)} %bitcast.51), calls=%async_computation.9 | async-start | bytes 7077888
  284.9 13.7 %copy-start.2 = (f32[200,1600]{1,0:T(8,128)S(1)}, f32[200,1600]{1,0:T(8,128)}, u32[]{:S(2)}) copy-start(f32[200,1600]{1,0:T(8,128)} %param.15) | copy-start | bytes 3840004
  284.9 13.7 %copy-start.3 = (bf16[200,1600]{1,0:T(8,128)(2,1)S(1)}, bf16[200,1600]{1,0:T(8,128)(2,1)}, u32[]{:S(2)}) copy-start(bf16[200,1600]{1,0:T(8,128)(2,1)} %param.13) | copy-start | bytes 1920004
  298.6 4.5 %copy-start.5 = (f32[1600]{0:T(1024)S(1)}, f32[1600]{0:T(1024)}, u32[]{:S(2)}) copy-start(f32[1600]{0:T(1024)} %param.16) | copy-start | bytes 19204
Sparse Core Ops, SparseCore 0:
  15.1 50.1 reduce-scatter.6
  68.5 28.7 reduce-scatter.8
  99.6 69.1 all-reduce.3
  171.2 70.1 all-gather.2
  302.2 38.9 all-gather.4

commit v7 on v6

--- a/solution.py
+++ b/solution.py
@@ -27,8 +27,13 @@
     own_rows = corrected.shape[0]
     block = own_rows + 24
     padding = jnp.zeros((block - own_rows - 1, corrected.shape[1]), jnp.float32)
-    z_summed = lax.psum(jnp.concatenate([corrected, column_sums[None, :], padding], axis=0), "gz")
-    piece = lax.psum_scatter(z_summed, "gx", scatter_dimension=0, tiled=True)
+    x_piece = lax.psum_scatter(
+        jnp.concatenate([corrected, column_sums[None, :], padding], axis=0),
+        "gx",
+        scatter_dimension=0,
+        tiled=True,
+    )
+    piece = jnp.sum(lax.all_gather(x_piece, "gz", axis=0), axis=0)
     extended = lax.all_gather(piece, ("shard", "gx"), axis=0, tiled=True)
     all_sums = jnp.sum(extended.reshape(shard_count, block, -1)[:, own_rows], axis=0)
     is_total_row = (jnp.arange(shard_count * block) % block < own_rows)[:, None]

time: 355 us -> 313 us (0.88)
  waiting for transfers between devices: 259 us -> 227 us
  matrix products: 60.5 us -> 47.7 us
  other arithmetic: 18.2 us -> 22.5 us
    psum x1 -> x0, waiting for transfers between devices: 71.5 us -> none  [shards(): lax.psum(jnp.concatenate([corrected, column_sums[None, :], padding], axis...]
    all_gather x0 -> x1, waiting for transfers between devices: none -> 45.2 us  [shards(): piece = jnp.sum(lax.all_gather(x_piece, 'gz', axis=0), axis=0)]
    dot_general x2, matrix products: 27.4 us -> 15 us  [shards(): lax.dot_general(extended, ortho, (((0,), (0,)), ((), ())), precision=high)]
    all_gather x1, waiting for transfers between devices: 72.6 us -> 66.5 us  [shards(): extended = lax.all_gather(piece, ('shard', 'gx'), axis=0, tiled=True)]
where the time goes in v7:
time: 313 us
  waiting for transfers between devices  227 us (73%)
  matrix products  47.7 us (15%)
  other arithmetic  22.5 us (7%)
  between operations  13.9 us (4%)
    unnamed x7, waiting for transfers between devices  77.5 us
    all_gather x1, waiting for transfers between devices, shards(): extended = lax.all_gather(piece, ('shard', 'gx'), axis=0, tiled=True)  66.5 us
    all_gather x1, waiting for transfers between devices, shards(): piece = jnp.sum(lax.all_gather(x_piece, 'gz', axis=0), axis=0)  45.2 us
    all_gather x1, waiting for transfers between devices, shards(): lax.all_gather(new_weight, 'shard', axis=0, tiled=True)  37.5 us
    dot_general x2, matrix products, shards(): lax.dot_general(extended, ortho, (((0,), (0,)), ((), ())), precision=high)  15 us
    dot_general x2, matrix products, shards(): jnp.dot(extended, basis, precision=high)  14.3 us
    dot_general x1, matrix products, shards(): jnp.dot(next_inputs, lax.all_gather(new_weight, 'shard', axis=0, tiled=Tr...  7.35 us
    another operation x6, other arithmetic, shards(): lower_factor = jnp.linalg.cholesky(gram)  7.2 us
  transfers between devices with their start and end apart: 5, of which 5 were waited for; matrix products, arithmetic and copies ran while one was open for 1% of the time, Pallas kernels for 0%

profile of v7, /device:TPU:1, one launch (start us, length us, event | category | flops | bytes accessed | tf_op | source)
XLA Modules:
  0.0 313.2 jit_solution(17984482258544204629)
XLA Ops:
  7.2 0.0 copy-start
  7.2 0.0 reduce-scatter.7.cloned.1.call-start
  7.2 1.4 copy-done
  8.6 6.3 %convolution_convert_fusion = bf16[1600,1600]{1,0:T(8,128)(2,1)} fusion(bf16[512,1600]{0,1:T(8,128)(2,1)S(1)} %copy-done, bf16[512,1600]{0,1:T(8,128)(2,1)} %param.12), kind=kOutput, calls=%fused_computation | convolution fusion | flops 2624000000 | bytes 8396800 | tf_op jit(solution)/shard_map/dot_general | solution.py:18
  14.9 0.0 reduce-scatter.7.cloned.1.call-update
  14.9 0.0 reduce-scatter.9.cloned.1.call-start
  15.0 1.7 convert_reduce_fusion
  16.8 0.1 pad.2.clone
  16.8 48.5 %reduce-scatter.7.cloned.1.call-done = bf16[200,1600]{1,0:T(8,128)(2,1)} async-done(((bf16[1600,1600]{1,0:T(8,128)(2,1)}), bf16[200,1600]{1,0:T(8,128)(2,1)}) %reduce-scatter.7.cloned.1.call-update) | async-done | bytes 640016
  65.3 1.6 bitcast_add_fusion
  66.9 1.3 maximum_maximum_fusion
  68.2 0.0 reduce-scatter.9.cloned.1.call-update
  68.2 0.0 all-gather.9.cloned.1.call-start
  68.3 28.9 %reduce-scatter.9.cloned.1.call-done = f32[56,1600]{1,0:T(8,128)} async-done(((f32[224,1600]{1,0:T(8,128)}), f32[56,1600]{1,0:T(8,128)}) %reduce-scatter.9.cloned.1.call-update) | async-done | bytes 358416
  97.2 0.0 all-gather.9.cloned.1.call-update
  97.2 0.0 all-gather.5.cloned.1.call-start
  97.3 45.2 %all-gather.9.cloned.1.call-done = f32[448,1600]{1,0:T(8,128)} async-done(((f32[56,1600]{1,0:T(8,128)}), f32[448,1600]{1,0:T(8,128)}) %all-gather.9.cloned.1.call-update) | async-done | bytes 2867216 | tf_op jit(solution)/shard_map/all_gather | solution.py:36
  142.5 2.8 reduce_sum.28
  145.3 0.0 all-gather.5.cloned.1.call-update
  145.3 0.2 all-gather.7.cloned.1.call-start
  145.6 66.5 %all-gather.5.cloned.1.call-done = f32[1792,1600]{1,0:T(8,128)} async-done(((f32[56,1600]{1,0:T(8,128)}), f32[1792,1600]{1,0:T(8,128)}) %all-gather.5.cloned.1.call-update) | async-done | bytes 11468816 | tf_op jit(solution)/shard_map/all_gather | solution.py:37
  212.1 9.2 %convolution_select_fusion.1 = f32[1792,32]{0,1:T(8,128)S(1)} fusion(f32[1792,1600]{1,0:T(8,128)} %all-gather.5.cloned.1.call-done, f32[1600,32]{0,1:T(8,128)S(1)} %copy-done.4, pred[1792]{0:T(1024)(128)(4,1)S(1)} %fusion.15), kind=kOutput, calls=%fused_computation.7 | convolution fusion | flops 550559744 | bytes 11904768 | tf_op jit(solution)/shard_map/dot_general | solution.py:43
  221.3 0.3 fusion.22
  221.6 0.1 copy.18
  221.7 2.9 cholesky.44
  224.7 0.6 compare_reduce_fusion.1
  225.3 0.7 fusion.7
  226.0 2.4 custom-call.6
  228.4 0.4 fusion.3
  228.8 7.5 %convolution_multiply_fusion.1 = f32[1600,32]{0,1:T(8,128)S(1)} fusion(f32[1792,1600]{1,0:T(8,128)} %all-gather.5.cloned.1.call-done, f32[32,1792]{1,0:T(8,128)S(1)} %fusion.3), kind=kOutput, calls=%fused_computation.5 | convolution fusion | flops 550553600 | bytes 11902976 | tf_op jit(solution)/shard_map/dot_general | solution.py:48
  236.4 0.2 copy-done.1
  236.6 5.0 %convolution_select_fusion = f32[1792,32]{0,1:T(8,128)S(1)} fusion(f32[1792,1600]{1,0:T(8,128)S(1)} %copy-done.1, f32[1600,32]{0,1:T(8,128)S(1)} %convolution_multiply_fusion.1, pred[1792]{0:T(1024)(128)(4,1)S(1)} %fusion.15), kind=kOutput, calls=%fused_computation.6 | convolution fusion | flops 550559744 | bytes 11904768 | tf_op jit(solution)/shard_map/dot_general | solution.py:43
  241.7 0.3 fusion.23
  242.0 0.1 copy.19
  242.1 2.9 cholesky.55
  245.0 0.6 compare_reduce_fusion
  245.7 0.7 fusion.8
  246.4 2.4 custom-call.7
  248.8 0.4 fusion.1
  249.2 0.0 copy-start.2
  249.2 7.5 %convolution_multiply_fusion = f32[1600,32]{0,1:T(8,128)S(1)} fusion(f32[1792,1600]{1,0:T(8,128)} %all-gather.5.cloned.1.call-done, f32[32,1792]{1,0:T(8,128)S(1)} %fusion.1), kind=kOutput, calls=%fused_computation.4 | convolution fusion | flops 550553600 | bytes 11902976 | tf_op jit(solution)/shard_map/dot_general | solution.py:48
  256.8 0.0 copy-start.5
  256.8 3.4 %subtract_convert_fusion = (bf16[200,1600]{1,0:T(8,128)(2,1)}, f32[200,1600]{1,0:T(8,128)}, f32[1,200,1600]{2,1,0:T(8,128)}) fusion(bf16[200,1600]{1,0:T(8,128)(2,1)S(1)} %copy-done.3, f32[200,1600]{1,0:T(8,128)S(1)} %copy-done.2, f32[200,1600]{1,0:T(8,128)S(1)} %bitcast_add_fusion, f32[1600,32]{0,1:T(8,128)S(1)} %convolution_multiply_fusion, ...), kind=kOutput, calls=%fused_computation.11 | convolution fusion | flops 125120000 | bytes 6773764 | tf_op jit(solution)/shard_map/dot_general | solution.py:52
  260.1 0.0 all-gather.7.cloned.1.call-update
  260.1 1.0 slice_reduce_fusion
  261.2 0.6 multiply_add_fusion.1
  261.8 37.5 %all-gather.7.cloned.1.call-done = bf16[1600,1600]{1,0:T(8,128)(2,1)} async-done(((bf16[200,1600]{1,0:T(8,128)(2,1)}), bf16[1600,1600]{1,0:T(8,128)(2,1)}) %all-gather.7.cloned.1.call-update) | async-done | bytes 5120016 | tf_op jit(solution)/shard_map/all_gather | solution.py:59
  299.3 7.4 %fusion = bf16[512,1600]{0,1:T(8,128)(2,1)} fusion(bf16[1600,1600]{1,0:T(8,128)(2,1)} %all-gather.7.cloned.1.call-done, bf16[512,1600]{0,1:T(8,128)(2,1)} %param.18), kind=kOutput, calls=%fused_computation.3 | convolution fusion | flops 2622259200 | bytes 8396800 | tf_op jit(solution)/shard_map/dot_general | solution.py:57
  (14 shorter events, 0.1 us)
Async XLA Ops:
  7.2 1.4 copy-start
  7.2 58.1 %reduce-scatter.7.cloned.1.call-start = ((), (), s32[]{:S(2)}) async-start(), calls=%async_computation.5 | async-start | bytes 5990400
  14.9 82.2 %reduce-scatter.9.cloned.1.call-start = ((), (), s32[]{:S(2)}) async-start(), calls=%async_computation.6 | async-start | bytes 1863680
  68.2 74.3 %all-gather.9.cloned.1.call-start = ((), (), s32[]{:S(2)}) async-start(), calls=%async_computation.4 | async-start | bytes 3354624 | tf_op jit(solution)/shard_map/all_gather | solution.py:36
  97.2 114.8 %all-gather.5.cloned.1.call-start = ((), (), s32[]{:S(2)}) async-start(), calls=%async_computation.2 | async-start | bytes 12300288 | tf_op jit(solution)/shard_map/all_gather | solution.py:37
  142.5 69.6 %copy-start.4 = (f32[1600,32]{0,1:T(8,128)S(1)}, f32[1600,32]{0,1:T(8,128)}, u32[]{:S(2)}) copy-start(f32[1600,32]{0,1:T(8,128)} %param.17) | copy-start | bytes 614404
  145.3 154.0 %all-gather.7.cloned.1.call-start = ((), (), s32[]{:S(2)}) async-start(), calls=%async_computation.3 | async-start | bytes 5990400 | tf_op jit(solution)/shard_map/all_gather | solution.py:59
  228.8 7.8 %copy-start.1 = (f32[1792,1600]{1,0:T(8,128)S(1)}, f32[1792,1600]{1,0:T(8,128)}, u32[]{:S(2)}) copy-start(f32[1792,1600]{1,0:T(8,128)} %all-gather.5.cloned.1.call-done) | copy-start | bytes 34406404
  249.2 7.5 %copy-start.2 = (f32[200,1600]{1,0:T(8,128)S(1)}, f32[200,1600]{1,0:T(8,128)}, u32[]{:S(2)}) copy-start(f32[200,1600]{1,0:T(8,128)} %param.15) | copy-start | bytes 3840004
  249.2 7.5 %copy-start.3 = (bf16[200,1600]{1,0:T(8,128)(2,1)S(1)}, bf16[200,1600]{1,0:T(8,128)(2,1)}, u32[]{:S(2)}) copy-start(bf16[200,1600]{1,0:T(8,128)(2,1)} %param.13) | copy-start | bytes 1920004
  256.8 4.4 %copy-start.5 = (f32[1600]{0:T(1024)S(1)}, f32[1600]{0:T(1024)}, u32[]{:S(2)}) copy-start(f32[1600]{0:T(1024)} %param.16) | copy-start | bytes 19204
Sparse Core Ops, SparseCore 0:
  15.1 50.1 reduce-scatter.6
  68.4 28.7 reduce-scatter.8
  99.0 43.4 all-gather.8
  145.5 66.5 all-gather.4
  260.3 38.9 all-gather.6
